TPU v7x, 512 devices: a whole 4x4x16 slice. The times are simulated.
512 devices in a mesh: grp: 4 (over y), seq: 32 (over z, core), mp: 4 (over x).
Axes of the slice: x: 4, y: 4, z: 16, core: 2. Of those that a mesh axis runs over, the one named last changes fastest.
Arguments:
- queries: bfloat16 [4, 4096, 2048], P('grp', 'seq', 'mp'), may hold values from -16 to 16
- d_out: bfloat16 [4, 4096, 2048], P('grp', 'seq', 'mp'), may hold values from -6 to 6
- neighbour_kv: bfloat16 [4, 256, 128, 2, 2048], P('grp', 'seq', None, None, 'mp'), may hold values from -16 to 16
- target: int32 [4, 256], P('grp', 'seq'), may hold values from -1 to 127, as said below
- bias: float32 [16, 191], P('mp'), may hold values from -6 to 6
Outputs:
- attended: bfloat16 [4, 4096, 2048], P('grp', 'seq', 'mp')
- d_query: bfloat16 [4, 4096, 2048], P('grp', 'seq', 'mp')
- d_kv: bfloat16 [4, 256, 128, 2, 2048], P('grp', 'seq', None, None, 'mp')
- d_bias: float32 [16, 191], P('mp')
Inputs may be any that keep to these rules, and one draw needn't show every extreme that they name: `target`: in each group every entry 0..127 stands in exactly one slot and -1 marks an empty slot. The slots of one index of seq hold at most 1 entries e with the same e // 4, and some index reaches that; some index of seq holds 8 entries.
All inputs are finite; a program needn't handle non-finite values.
Results may differ from a plain program's by a relative error of at most 0.011.
Values may be sent and summed in bfloat16 or wider, within the bound.
No kernel may reach another device: no remote copies, remote signals or barrier semaphores. Data moves between devices by JAX's collectives and lax.ppermute only.
A program may use at most 128 MiB of HBM per device.

v0:
```python
import jax
import jax.numpy as jnp
from jax import lax
from jax.sharding import PartitionSpec as P

STRETCH = 64
NB_LEN = 128


def passed_along(block, axis, distance):
    devices = range(lax.axis_size(axis))
    route = [(i - distance, i) for i in devices if i - distance in devices]
    return lax.ppermute(block, axis, route)


def bias_grid(lookup, row_count, col_count):
    head_num = lookup.shape[0]
    span = row_count + col_count
    padded = jnp.pad(lookup, ((0, 0), (0, 1)))
    flattened = jnp.tile(padded, (1, row_count))
    flattened = jnp.pad(flattened, ((0, 0), (0, row_count)))
    shaped = flattened.reshape(head_num, row_count, span + 1)[:, :, :col_count]
    return shaped[:, :, ::-1]


def bias_fold(grads):
    head_num, row_count, col_count = grads.shape
    turned = grads[:, :, ::-1]
    padded = jnp.pad(turned, ((0, 0), (0, 0), (0, row_count)))
    flattened = padded.reshape(head_num, row_count * (row_count + col_count))
    flattened = flattened[:, : row_count * (row_count + col_count - 1)]
    return jnp.sum(flattened.reshape(head_num, row_count, row_count + col_count - 1), axis=1)


def select_rows(picker, lookup):
    chosen = jnp.dot(
        picker.astype(lookup.dtype),
        lookup,
        preferred_element_type=jnp.float32,
        precision=lax.Precision.HIGHEST,
    )
    return chosen.astype(lookup.dtype)


def slot_places(target_row, owners, capacity, per_owner):
    is_used = target_row >= 0
    owner_of = jnp.where(is_used, target_row // per_owner, -1)
    positions = jnp.arange(target_row.shape[0])
    earlier = (
        (positions[None, :] < positions[:, None])
        & (owner_of[None, :] == owner_of[:, None])
        & is_used[None, :]
    )
    rank_of = jnp.sum(earlier.astype(jnp.int32), axis=1)
    match_owner = owner_of[None, :] == jnp.arange(owners)[:, None]
    match_rank = rank_of[None, :] == jnp.arange(capacity)[:, None]
    return match_owner[:, None, :] & match_rank[None, :, :] & is_used[None, None, :]


def local(queries, d_out, neighbour_kv, target, bias):
    tok_rows = queries.shape[1]
    width_dev = queries.shape[2]
    head_count = bias.shape[0]
    head_depth = width_dev // head_count
    stretch_count = tok_rows // STRETCH
    per_owner = 2 * stretch_count
    shard_count = lax.axis_size("seq")
    my_index = lax.axis_index("seq")
    group_size = min(shard_count, per_owner)
    capacity = (per_owner + group_size - 1) // group_size
    seq_stretches = min(2048, tok_rows * shard_count) // STRETCH
    scale_factor = head_depth ** (-0.5)
    bias_rows = bias_grid(bias, STRETCH, NB_LEN).transpose(1, 0, 2)
    q_rows = queries[0]
    g_rows = d_out[0]
    next_pair = passed_along(jnp.stack([q_rows[:STRETCH], g_rows[:STRETCH]]), "seq", -1)
    row_ids = jnp.arange(STRETCH)
    stretch_ids = my_index * stretch_count + jnp.arange(stretch_count)
    is_live = (row_ids[None, :] == 0) | ((stretch_ids[:, None] + 1) % seq_stretches != 0)
    live_rows = is_live.astype(jnp.float32)
    q_win = jnp.concatenate([q_rows, next_pair[0]])[STRETCH - 1 : STRETCH - 1 + tok_rows]
    q_win = q_win.reshape(stretch_count, STRETCH * width_dev)
    g_win = jnp.concatenate([g_rows, next_pair[1]])[STRETCH - 1 : STRETCH - 1 + tok_rows]
    g_win = g_win.reshape(stretch_count, STRETCH, width_dev) * is_live[:, :, None].astype(
        jnp.bfloat16
    )
    g_win = g_win.reshape(stretch_count, STRETCH * width_dev)
    my_targets = target[0]
    slot_count = my_targets.shape[0]
    send_map = slot_places(my_targets, shard_count, capacity, per_owner)
    id_buffer = jnp.sum(jnp.where(send_map, my_targets[None, None, :] + 1, 0), axis=2) - 1
    recv_ids = lax.all_to_all(id_buffer, "seq", split_axis=0, concat_axis=0, tiled=True)
    flat_ids = recv_ids.reshape(shard_count * capacity)
    has_entry = flat_ids >= 0
    local_entry = flat_ids - my_index * per_owner
    entry_pick = (local_entry[:, None] == jnp.arange(per_owner)[None, :]) & has_entry[:, None]
    stretch_pick = (local_entry[:, None] // 2 == jnp.arange(stretch_count)[None, :]) & has_entry[
        :, None
    ]
    back_pick = send_map.reshape(shard_count * capacity, slot_count)
    slot_pick = back_pick.T
    q_send = select_rows(stretch_pick, q_win).reshape(shard_count, capacity, STRETCH * width_dev)
    g_send = select_rows(stretch_pick, g_win).reshape(shard_count, capacity, STRETCH * width_dev)
    q_recv, g_recv = (
        lax.all_to_all(q_send, "seq", split_axis=0, concat_axis=0, tiled=True),
        lax.all_to_all(g_send, "seq", split_axis=0, concat_axis=0, tiled=True),
    )
    q_slots = select_rows(slot_pick, q_recv.reshape(shard_count * capacity, -1))
    q_slots = q_slots.reshape(slot_count, STRETCH, head_count, head_depth)
    stored = neighbour_kv[0]
    key_rows = stored[:, :, 0].reshape(slot_count, NB_LEN, head_count, head_depth)
    value_rows = stored[:, :, 1].reshape(slot_count, NB_LEN, head_count, head_depth)
    scores = jnp.einsum("sihd,sjhd->sihj", q_slots, key_rows, preferred_element_type=jnp.float32)
    scores = scores * scale_factor + bias_rows[None]
    peak_val = jnp.max(scores, axis=-1)
    weights = jnp.exp(scores - peak_val[..., None])
    row_total = jnp.sum(weights, axis=-1)
    partial_value = jnp.einsum(
        "sihj,sjhd->sihd",
        weights.astype(jnp.bfloat16),
        value_rows,
        preferred_element_type=jnp.float32,
    )
    part_send = select_rows(back_pick, partial_value.reshape(slot_count, -1)).reshape(
        shard_count, capacity, -1
    )
    peak_send = select_rows(back_pick, peak_val.reshape(slot_count, -1)).reshape(
        shard_count, capacity, -1
    )
    total_send = select_rows(back_pick, row_total.reshape(slot_count, -1)).reshape(
        shard_count, capacity, -1
    )
    part_recv, peak_recv, total_recv = (
        lax.all_to_all(part_send, "seq", split_axis=0, concat_axis=0, tiled=True),
        lax.all_to_all(peak_send, "seq", split_axis=0, concat_axis=0, tiled=True),
        lax.all_to_all(total_send, "seq", split_axis=0, concat_axis=0, tiled=True),
    )
    entry_back = entry_pick.T
    parts_own = select_rows(entry_back, part_recv.reshape(shard_count * capacity, -1))
    parts_own = parts_own.reshape(stretch_count, 2, STRETCH, head_count, head_depth)
    peaks_own = select_rows(entry_back, peak_recv.reshape(shard_count * capacity, -1))
    peaks_own = peaks_own.reshape(stretch_count, 2, STRETCH, head_count)
    totals_own = select_rows(entry_back, total_recv.reshape(shard_count * capacity, -1))
    totals_own = totals_own.reshape(stretch_count, 2, STRETCH, head_count)
    top_peak = jnp.max(peaks_own, axis=1)
    factor = jnp.exp(peaks_own - top_peak[:, None])
    denominator = jnp.sum(factor * totals_own, axis=1)
    combined = jnp.sum(factor[..., None] * parts_own, axis=1) / denominator[..., None]
    combined = combined * live_rows[:, :, None, None]
    att_win = combined.astype(jnp.bfloat16).reshape(tok_rows, width_dev)
    att_before = passed_along(att_win[tok_rows - STRETCH :], "seq", 1)
    log_total = top_peak + jnp.log(denominator)
    g_wide = g_win.reshape(stretch_count, STRETCH, head_count, head_depth).astype(jnp.float32)
    inner_dot = jnp.sum(g_wide * combined, axis=-1)
    row_stats = jnp.repeat(jnp.stack([log_total, inner_dot], axis=1), 2, axis=0)
    stats_send = select_rows(entry_pick, row_stats.reshape(per_owner, -1)).reshape(
        shard_count, capacity, -1
    )
    stats_recv = lax.all_to_all(stats_send, "seq", split_axis=0, concat_axis=0, tiled=True)
    g_slots = select_rows(slot_pick, g_recv.reshape(shard_count * capacity, -1))
    g_slots = g_slots.reshape(slot_count, STRETCH, head_count, head_depth)
    stats_slots = select_rows(slot_pick, stats_recv.reshape(shard_count * capacity, -1))
    stats_slots = stats_slots.reshape(slot_count, 2, STRETCH, head_count)
    prob_full = jnp.exp(scores - stats_slots[:, 0][..., None])
    prob_low = prob_full.astype(jnp.bfloat16)
    grad_values = jnp.einsum(
        "sihj,sihd->sjhd", prob_low, g_slots, preferred_element_type=jnp.float32
    )
    grad_prob = jnp.einsum(
        "sihd,sjhd->sihj", g_slots, value_rows, preferred_element_type=jnp.float32
    )
    grad_scores = prob_full * (grad_prob - stats_slots[:, 1][..., None])
    scores_low = grad_scores.astype(jnp.bfloat16)
    grad_rows = (
        jnp.einsum("sihj,sjhd->sihd", scores_low, key_rows, preferred_element_type=jnp.float32)
        * scale_factor
    )
    grad_keys = (
        jnp.einsum("sihj,sihd->sjhd", scores_low, q_slots, preferred_element_type=jnp.float32)
        * scale_factor
    )
    d_kv = jnp.stack(
        [
            grad_keys.reshape(slot_count, NB_LEN, width_dev),
            grad_values.reshape(slot_count, NB_LEN, width_dev),
        ],
        axis=2,
    ).astype(jnp.bfloat16)
    bias_part = bias_fold(jnp.sum(grad_scores, axis=0).transpose(1, 0, 2))
    rows_send = select_rows(back_pick, grad_rows.reshape(slot_count, -1)).reshape(
        shard_count, capacity, -1
    )
    rows_recv = lax.all_to_all(rows_send, "seq", split_axis=0, concat_axis=0, tiled=True)
    grad_entries = select_rows(entry_back, rows_recv.reshape(shard_count * capacity, -1))
    grad_entries = grad_entries.reshape(stretch_count, 2, STRETCH * width_dev)
    grad_win = (
        (grad_entries[:, 0] + grad_entries[:, 1]).astype(jnp.bfloat16).reshape(tok_rows, width_dev)
    )
    grad_before = passed_along(grad_win[tok_rows - STRETCH :], "seq", 1)
    attended = jnp.concatenate([att_before[1:], att_win[: tok_rows - STRETCH + 1]])
    d_query = jnp.concatenate([grad_before[1:], grad_win[: tok_rows - STRETCH + 1]])
    raw_sum = lax.psum(bias_part, ("grp", "seq"))
    squares = lax.psum(jnp.sum(raw_sum * raw_sum), "mp")
    d_bias = raw_sum * jnp.minimum(1.0, 1.0 / jnp.sqrt(squares + 1e-12))
    return (attended[None], d_query[None], d_kv[None], d_bias)


def solution(mesh):
    in_specs = (
        P("grp", "seq", "mp"),
        P("grp", "seq", "mp"),
        P("grp", "seq", None, None, "mp"),
        P("grp", "seq"),
        P("mp", None),
    )
    out_specs = (
        P("grp", "seq", "mp"),
        P("grp", "seq", "mp"),
        P("grp", "seq", None, None, "mp"),
        P("mp", None),
    )
    return jax.shard_map(local, mesh=mesh, in_specs=in_specs, out_specs=out_specs, check_vma=False)
```

profile of v0, /device:TPU:1, one launch (start us, length us, event | category | flops | bytes accessed | tf_op | source)
XLA Modules:
  0.0 1025.3 jit_solution(9001594490378168722)
XLA Ops:
  4.3 16.7 %all-to-all-start = ((s32[32,1,1]{2,1,0:T(1,128)}), s32[32,1,1]{2,1,0:T(1,128)S(1)}, u32[]{:S(2)}, u32[]{:S(2)}) async-start(s32[32,1,1]{2,1,0:T(1,128)} %copy.156), calls=%async_computation | async-start | bytes 32768 | tf_op jit(solution)/shard_map/all_to_all | solution.py:92
  24.9 7.8 all-to-all-done
  39.3 4.5 reshape.685
  43.8 6.9 all-to-all-start.1
  53.3 4.5 reduce.10
  57.8 4.5 reshape.687
  62.3 87.0 %all-to-all-done.1 = bf16[32,2,16384]{2,1,0:T(2,128)(2,1)S(1)} async-done(((bf16[32,2,16384]{2,1,0:T(2,128)(2,1)}), bf16[32,2,16384]{2,1,0:T(2,128)(2,1)S(1)}, u32[]{:S(2)}, u32[]{:S(2)}) %all-to-all-start.1) | async-done | bytes 2097184 | tf_op jit(solution)/shard_map/all_to_all | solution.py:105
  149.3 5.2 all-to-all-start.6
  154.5 6.2 copy.158
  164.1 10.5 %reshape.686 = bf16[32,1,32768]{2,1,0:T(2,128)(2,1)} reshape(bf16[32,2,16384]{2,1,0:T(2,128)(2,1)} %copy-done) | data formatting | bytes 4194304
  184.6 69.2 %all-to-all-done.6 = bf16[32,2,16384]{2,1,0:T(2,128)(2,1)} async-done(((bf16[32,2,16384]{2,1,0:T(2,128)(2,1)}), bf16[32,2,16384]{2,1,0:T(2,128)(2,1)}, u32[]{:S(2)}, u32[]{:S(2)}) %all-to-all-start.6) | async-done | bytes 2097184 | tf_op jit(solution)/shard_map/all_to_all | solution.py:106
  253.8 6.3 all-to-all-start.2
  267.3 5.0 all-to-all-done.2
  272.3 7.3 all-to-all-start.4
  282.7 6.3 copy.168
  291.7 9.9 all-to-all-start.3
  301.7 10.5 %reshape.688 = bf16[32,1,32768]{2,1,0:T(2,128)(2,1)} reshape(bf16[32,2,16384]{2,1,0:T(2,128)(2,1)} %all-to-all-done.6) | data formatting | bytes 4194304
  313.4 171.4 %all-to-all-done.3 = f32[32,1,32768]{2,1,0:T(1,128)} async-done(((f32[32,1,32768]{2,1,0:T(1,128)}), f32[32,1,32768]{2,1,0:T(1,128)}, u32[]{:S(2)}, u32[]{:S(2)}) %all-to-all-start.3) | async-done | bytes 4194336 | tf_op jit(solution)/shard_map/all_to_all | solution.py:134
  484.7 6.6 copy.249
  491.3 6.0 dot_general.86
  497.4 6.8 fusion.20
  506.6 10.9 %all-to-all-start.5 = ((f32[32,1,512]{2,1,0:T(1,128)}), f32[32,1,512]{2,1,0:T(1,128)S(1)}, u32[]{:S(2)}, u32[]{:S(2)}) async-start(f32[32,1,512]{2,1,0:T(1,128)} %copy.177), calls=%async_computation.5 | async-start | bytes 131072 | tf_op jit(solution)/shard_map/all_to_all | solution.py:159
  517.5 4.5 convolution_convert_fusion.2
  522.0 8.5 all-to-all-done.5
  540.1 6.3 copy.187
  546.4 6.1 all-to-all-start.7
  556.7 169.2 %collective-permute-done.1 = bf16[64,512]{1,0:T(8,128)(2,1)S(1)} collective-permute-done((bf16[64,512]{1,0:T(8,128)(2,1)S(1)}, bf16[64,512]{1,0:T(8,128)(2,1)S(1)}, u32[]{:S(2)}, u32[]{:S(2)}) %collective-permute-start.1) | collective-permute-done | bytes 65568 | tf_op jit(solution)/shard_map/ppermute | solution.py:13
  726.5 256.5 %psum.14 = f32[4,191]{1,0:T(4,128)S(1)} all-reduce(f32[4,191]{1,0:T(4,128)S(1)} %reduce_sum.88), channel_id=1, replica_groups=mesh['grp'=4,'seq'=32,'mp'=4] {'grp','seq'}, use_global_device_ids=true, to_apply=%region_10.11 | all-reduce | flops 764 | bytes 6112 | tf_op jit(solution)/shard_map/psum | solution.py:202
  984.3 9.1 psum.15
  995.2 4.6 copy.191
  1006.1 6.7 pad_maximum_fusion
  1012.8 6.0 fusion.2
  (131 shorter events, 75.8 us)
Async XLA Ops:
  4.3 28.5 %all-to-all-start = ((s32[32,1,1]{2,1,0:T(1,128)}), s32[32,1,1]{2,1,0:T(1,128)S(1)}, u32[]{:S(2)}, u32[]{:S(2)}) async-start(s32[32,1,1]{2,1,0:T(1,128)} %copy.156), calls=%async_computation | async-start | bytes 32768 | tf_op jit(solution)/shard_map/all_to_all | solution.py:92
  22.7 11.4 %collective-permute-start = (bf16[2,64,512]{2,1,0:T(8,128)(2,1)S(1)}, bf16[2,64,512]{2,1,0:T(8,128)(2,1)S(1)}, u32[]{:S(2)}, u32[]{:S(2)}) collective-permute-start(bf16[2,64,512]{2,1,0:T(8,128)(2,1)S(1)} %pad_maximum_fusion.3), channel_id=1, source_target_pairs={{4,0},{8,4},{12,8},{16,12},{20,16},{24,20},{28,24},{32,28},{36,32}... | collective-permute-start | bytes 393224 | tf_op jit(solution)/shard_map/ppermute | solution.py:13
  39.3 11.7 %copy-start.5 = (bf16[1,128,512]{2,1,0:T(8,128)(2,1)S(1)}, bf16[1,128,512]{2,1,0:T(8,128)(2,1)}, u32[]{:S(2)}) copy-start(bf16[1,128,512]{2,1,0:T(8,128)(2,1)} %param.6) | copy-start | bytes 393220
  43.8 105.5 %all-to-all-start.1 = ((bf16[32,2,16384]{2,1,0:T(2,128)(2,1)}), bf16[32,2,16384]{2,1,0:T(2,128)(2,1)S(1)}, u32[]{:S(2)}, u32[]{:S(2)}) async-start(bf16[32,2,16384]{2,1,0:T(2,128)(2,1)} %reshape.685), calls=%async_computation.1 | async-start | bytes 4194304 | tf_op jit(solution)/shard_map/all_to_all | solution.py:105
  62.3 98.4 %copy-start.7 = (f32[4,191]{1,0:T(4,128)S(1)}, f32[4,191]{1,0:T(4,128)}, u32[]{:S(2)}) copy-start(f32[4,191]{1,0:T(4,128)} %param.9) | copy-start | bytes 9172
  149.3 11.4 %copy-start = (bf16[32,2,16384]{2,1,0:T(2,128)(2,1)}, bf16[32,2,16384]{2,1,0:T(2,128)(2,1)S(1)}, u32[]{:S(2)}) copy-start(bf16[32,2,16384]{2,1,0:T(2,128)(2,1)S(1)} %all-to-all-done.1) | copy-start | bytes 6291460
  149.3 104.5 %all-to-all-start.6 = ((bf16[32,2,16384]{2,1,0:T(2,128)(2,1)}), bf16[32,2,16384]{2,1,0:T(2,128)(2,1)}, u32[]{:S(2)}, u32[]{:S(2)}) async-start(bf16[32,2,16384]{2,1,0:T(2,128)(2,1)} %reshape.687), calls=%async_computation.6 | async-start | bytes 4194304 | tf_op jit(solution)/shard_map/all_to_all | solution.py:106
  179.1 0.8 copy-start.4
  253.8 18.5 %all-to-all-start.2 = ((f32[32,1,256]{2,1,0:T(1,128)}), f32[32,1,256]{2,1,0:T(1,128)S(1)}, u32[]{:S(2)}, u32[]{:S(2)}) async-start(f32[32,1,256]{2,1,0:T(1,128)} %copy.162), calls=%async_computation.2 | async-start | bytes 65536 | tf_op jit(solution)/shard_map/all_to_all | solution.py:135
  272.3 19.4 %all-to-all-start.4 = ((f32[32,1,256]{2,1,0:T(1,128)}), f32[32,1,256]{2,1,0:T(1,128)S(1)}, u32[]{:S(2)}, u32[]{:S(2)}) async-start(f32[32,1,256]{2,1,0:T(1,128)} %copy.171), calls=%async_computation.4 | async-start | bytes 65536 | tf_op jit(solution)/shard_map/all_to_all | solution.py:136
  291.7 193.0 %all-to-all-start.3 = ((f32[32,1,32768]{2,1,0:T(1,128)}), f32[32,1,32768]{2,1,0:T(1,128)}, u32[]{:S(2)}, u32[]{:S(2)}) async-start(f32[32,1,32768]{2,1,0:T(1,128)} %copy.168), calls=%async_computation.3 | async-start | bytes 8388608 | tf_op jit(solution)/shard_map/all_to_all | solution.py:134
  506.6 23.9 %all-to-all-start.5 = ((f32[32,1,512]{2,1,0:T(1,128)}), f32[32,1,512]{2,1,0:T(1,128)S(1)}, u32[]{:S(2)}, u32[]{:S(2)}) async-start(f32[32,1,512]{2,1,0:T(1,128)} %copy.177), calls=%async_computation.5 | async-start | bytes 131072 | tf_op jit(solution)/shard_map/all_to_all | solution.py:159
  522.0 13.5 %copy-start.1 = (bf16[8,32768]{1,0:T(8,128)(2,1)}, bf16[8,32768]{1,0:T(8,128)(2,1)S(1)}, u32[]{:S(2)}) copy-start(bf16[8,32768]{1,0:T(8,128)(2,1)S(1)} %convolution_convert_fusion.2) | copy-start | bytes 1572868
  531.9 0.8 copy-start.3
  546.4 6.4 copy-start.6
  546.4 447.1 %copy-start.2 = (bf16[8,32768]{1,0:T(8,128)(2,1)S(1)}, bf16[8,32768]{1,0:T(8,128)(2,1)}, u32[]{:S(2)}) copy-start(bf16[8,32768]{1,0:T(8,128)(2,1)} %copy-done.1) | copy-start | bytes 1572868
  546.4 466.4 %all-to-all-start.7 = ((f32[32,1,32768]{2,1,0:T(1,128)}), f32[32,1,32768]{2,1,0:T(1,128)}, u32[]{:S(2)}, u32[]{:S(2)}) async-start(f32[32,1,32768]{2,1,0:T(1,128)} %copy.187), calls=%async_computation.7 | async-start | bytes 8388608 | tf_op jit(solution)/shard_map/all_to_all | solution.py:193
  552.9 173.0 %collective-permute-start.1 = (bf16[64,512]{1,0:T(8,128)(2,1)S(1)}, bf16[64,512]{1,0:T(8,128)(2,1)S(1)}, u32[]{:S(2)}, u32[]{:S(2)}) collective-permute-start(bf16[64,512]{1,0:T(8,128)(2,1)S(1)} %bitcast.224), channel_id=1, source_target_pairs={{0,4},{4,8},{8,12},{12,16},{16,20},{20,24},{24,28},{28,32},{32,36}... | collective-permute-start | bytes 196616 | tf_op jit(solution)/shard_map/ppermute | solution.py:13
  1020.3 4.2 collective-permute-start.2
where the time goes:
time: 1040 us; the launch traced here: 1030 us
  waiting for transfers between devices  522 us (50%)
  blocking collectives  266 us (26%)
  local copies, waits for them, and re-layouts  90.5 us (9%)
  starting transfers between devices  77.1 us (7%)
  matrix products  42.5 us (4%)
  other arithmetic  25.1 us (2%)
    psum x1, blocking collectives, local(): raw_sum = lax.psum(bias_part, ('grp', 'seq'))  257 us
    all_to_all x1, waiting for transfers between devices, local(): lax.all_to_all(part_send, 'seq', split_axis=0, concat_axis=0, tiled=True)  171 us
    ppermute x3, waiting for transfers between devices, passed_along(): return lax.ppermute(block, axis, route)  171 us
    all_to_all x1, waiting for transfers between devices, local(): lax.all_to_all(q_send, 'seq', split_axis=0, concat_axis=0, tiled=True)  87 us
    all_to_all x1, waiting for transfers between devices, local(): lax.all_to_all(g_send, 'seq', split_axis=0, concat_axis=0, tiled=True)  69.2 us
    unnamed x26, local copies, waits for them, and re-layouts  44.6 us
    dot_general x14, matrix products, select_rows(): jnp.dot(picker.astype(lookup.dtype), lookup, preferred_element_type=jnp.f...  32.4 us
  transfers between devices with their start and end apart: 11, of which 9 were waited for; matrix products, arithmetic and copies ran while one was open for 10% of the time, Pallas kernels for 0%

commit v1 on v0

v1 whole, which is shorter than its diff:
```python
import jax
import jax.numpy as jnp
from jax import lax
from jax.sharding import PartitionSpec as P

STRETCH = 64
NB_LEN = 128
SEQ_LEN = 2048


def passed_along(block, axis, distance):
    devices = range(lax.axis_size(axis))
    route = [(i - distance, i) for i in devices if i - distance in devices]
    return lax.ppermute(block, axis, route)


def bias_grid(lookup, row_count, col_count):
    head_num = lookup.shape[0]
    span = row_count + col_count
    padded = jnp.pad(lookup, ((0, 0), (0, 1)))
    flattened = jnp.tile(padded, (1, row_count))
    flattened = jnp.pad(flattened, ((0, 0), (0, row_count)))
    shaped = flattened.reshape(head_num, row_count, span + 1)[:, :, :col_count]
    return shaped[:, :, ::-1]


def bias_fold(grads):
    head_num, row_count, col_count = grads.shape
    turned = grads[:, :, ::-1]
    padded = jnp.pad(turned, ((0, 0), (0, 0), (0, row_count)))
    flattened = padded.reshape(head_num, row_count * (row_count + col_count))
    flattened = flattened[:, : row_count * (row_count + col_count - 1)]
    return jnp.sum(flattened.reshape(head_num, row_count, row_count + col_count - 1), axis=1)


def take_rows(table, index, valid):
    rows = jnp.take(table, index, axis=0)
    shape = (valid.shape[0],) + (1,) * (rows.ndim - 1)
    return jnp.where(valid.reshape(shape), rows, jnp.zeros((), rows.dtype))


def exchange(block):
    return lax.all_to_all(block, "seq", split_axis=0, concat_axis=0, tiled=True)


def local(queries, d_out, neighbour_kv, target, bias):
    tok_rows = queries.shape[1]
    width_dev = queries.shape[2]
    head_count = bias.shape[0]
    head_depth = width_dev // head_count
    stretch_count = tok_rows // STRETCH
    per_owner = 2 * stretch_count
    shard_count = lax.axis_size("seq")
    my_index = lax.axis_index("seq")
    group_rows = tok_rows * shard_count
    seq_stretches = min(SEQ_LEN, group_rows) // STRETCH
    scale_factor = head_depth ** (-0.5)
    bias_rows = bias_grid(bias, STRETCH, NB_LEN).transpose(1, 0, 2)
    row_ids = jnp.arange(STRETCH)

    q_all = lax.all_gather(queries[0], "seq", axis=0, tiled=True)
    g_all = lax.all_gather(d_out[0], "seq", axis=0, tiled=True)

    my_targets = target[0]
    slot_count = my_targets.shape[0]
    is_used = my_targets >= 0
    entry = jnp.where(is_used, my_targets, 0)
    stretch_of = entry // 2
    win_rows = stretch_of[:, None] * STRETCH + (STRETCH - 1) + row_ids[None, :]
    in_group = win_rows < group_rows
    win_rows = jnp.minimum(win_rows.reshape(-1), group_rows - 1)
    q_win = jnp.take(q_all, win_rows, axis=0).reshape(slot_count, STRETCH, width_dev)
    g_win = jnp.take(g_all, win_rows, axis=0).reshape(slot_count, STRETCH, width_dev)
    live_slot = (row_ids[None, :] == 0) | ((stretch_of[:, None] + 1) % seq_stretches != 0)
    q_keep = is_used[:, None] & in_group
    q_slots = jnp.where(q_keep[:, :, None], q_win, jnp.zeros((), q_win.dtype))
    g_slots = jnp.where((q_keep & live_slot)[:, :, None], g_win, jnp.zeros((), g_win.dtype))
    q_slots = q_slots.reshape(slot_count, STRETCH, head_count, head_depth)
    g_slots = g_slots.reshape(slot_count, STRETCH, head_count, head_depth)

    stored = neighbour_kv[0]
    key_rows = stored[:, :, 0].reshape(slot_count, NB_LEN, head_count, head_depth)
    value_rows = stored[:, :, 1].reshape(slot_count, NB_LEN, head_count, head_depth)
    scores = jnp.einsum("sihd,sjhd->sihj", q_slots, key_rows, preferred_element_type=jnp.float32)
    scores = scores * scale_factor + bias_rows[None]
    peak_val = jnp.max(scores, axis=-1)
    weights = jnp.exp(scores - peak_val[..., None])
    row_total = jnp.sum(weights, axis=-1)
    partial_value = jnp.einsum(
        "sihj,sjhd->sihd",
        weights.astype(jnp.bfloat16),
        value_rows,
        preferred_element_type=jnp.float32,
    )

    owner_of = jnp.where(is_used, my_targets // per_owner, -1)
    owner_match = owner_of[None, :] == jnp.arange(shard_count)[:, None]
    send_slot = jnp.argmax(owner_match, axis=1)
    send_has = jnp.any(owner_match, axis=1)
    part_send = take_rows(
        partial_value.astype(jnp.bfloat16).reshape(slot_count, STRETCH, width_dev), send_slot, send_has
    )
    slot_stats = jnp.concatenate(
        [
            jnp.stack([peak_val, row_total], axis=1).reshape(slot_count, -1),
            (entry + 1).astype(jnp.float32)[:, None],
        ],
        axis=1,
    )
    stat_send = take_rows(slot_stats, send_slot, send_has)
    part_recv = exchange(part_send)
    stat_recv = exchange(stat_send)

    own_entries = my_index * per_owner + jnp.arange(per_owner)
    sent_ids = stat_recv[:, -1].astype(jnp.int32) - 1
    where_held = sent_ids[None, :] == own_entries[:, None]
    held_by = jnp.argmax(where_held, axis=1)
    parts_own = jnp.take(part_recv, held_by, axis=0).astype(jnp.float32)
    parts_own = parts_own.reshape(stretch_count, 2, STRETCH, head_count, head_depth)
    stats_own = jnp.take(stat_recv[:, :-1], held_by, axis=0)
    stats_own = stats_own.reshape(stretch_count, 2, 2, STRETCH, head_count)
    peaks_own = stats_own[:, :, 0]
    totals_own = stats_own[:, :, 1]

    stretch_ids = my_index * stretch_count + jnp.arange(stretch_count)
    is_live = (row_ids[None, :] == 0) | ((stretch_ids[:, None] + 1) % seq_stretches != 0)
    live_rows = is_live.astype(jnp.float32)
    top_peak = jnp.max(peaks_own, axis=1)
    factor = jnp.exp(peaks_own - top_peak[:, None])
    denominator = jnp.sum(factor * totals_own, axis=1)
    combined = jnp.sum(factor[..., None] * parts_own, axis=1) / denominator[..., None]
    combined = combined * live_rows[:, :, None, None]
    att_win = combined.astype(jnp.bfloat16).reshape(tok_rows, width_dev)
    att_before = passed_along(att_win[tok_rows - STRETCH :], "seq", 1)

    g_dot = jnp.einsum(
        "sihd,sihd->sih", g_slots.astype(jnp.float32), partial_value, precision=lax.Precision.HIGHEST
    )
    mine = jnp.stack([peak_val, row_total, g_dot], axis=1)
    shared = jnp.concatenate(
        [mine.reshape(slot_count, -1), jnp.where(is_used, entry + 1, 0).astype(jnp.float32)[:, None]],
        axis=1,
    )
    shared_all = lax.all_gather(shared, "seq", tiled=True)
    partner = entry + 1 - 2 * (entry % 2)
    partner_at = jnp.argmax(shared_all[None, :, -1] == (partner + 1).astype(jnp.float32)[:, None], axis=1)
    theirs = jnp.take(shared_all[:, :-1], partner_at, axis=0).reshape(mine.shape)
    both_peak = jnp.maximum(mine[:, 0], theirs[:, 0])
    mine_f = jnp.exp(mine[:, 0] - both_peak)
    theirs_f = jnp.exp(theirs[:, 0] - both_peak)
    both_total = mine_f * mine[:, 1] + theirs_f * theirs[:, 1]
    lse_slots = both_peak + jnp.log(both_total)
    dd_slots = (mine_f * mine[:, 2] + theirs_f * theirs[:, 2]) / both_total
    dd_slots = jnp.where(is_used[:, None, None], dd_slots, 0.0)
    prob_full = jnp.exp(scores - lse_slots[..., None])
    prob_low = prob_full.astype(jnp.bfloat16)
    grad_prob = jnp.einsum(
        "sihd,sjhd->sihj", g_slots, value_rows, preferred_element_type=jnp.float32
    )
    grad_scores = prob_full * (grad_prob - dd_slots[..., None])
    scores_low = grad_scores.astype(jnp.bfloat16)
    grad_rows = (
        jnp.einsum("sihj,sjhd->sihd", scores_low, key_rows, preferred_element_type=jnp.float32)
        * scale_factor
    )
    mix_probs = jnp.stack([scores_low, prob_low], axis=1)
    mix_rows = jnp.stack([q_slots, g_slots], axis=1)
    grad_kv = jnp.einsum("sxihj,sxihd->sjxhd", mix_probs, mix_rows, preferred_element_type=jnp.float32)
    kv_scale = jnp.array([scale_factor, 1.0], jnp.float32)[None, None, :, None, None]
    d_kv = (grad_kv * kv_scale).astype(jnp.bfloat16).reshape(slot_count, NB_LEN, 2, width_dev)
    bias_part = bias_fold(jnp.sum(grad_scores, axis=0).transpose(1, 0, 2))

    dq_rows = jnp.zeros((shard_count, stretch_count, STRETCH, width_dev), jnp.bfloat16)
    dq_owner = jnp.where(is_used, owner_of, shard_count)
    dq_rows = dq_rows.at[dq_owner, stretch_of % stretch_count].set(
        grad_rows.astype(jnp.bfloat16).reshape(slot_count, STRETCH, width_dev), mode="drop"
    )
    grad_win = lax.psum_scatter(dq_rows, "seq", scatter_dimension=0, tiled=True)
    grad_win = grad_win.reshape(tok_rows, width_dev)
    grad_before = passed_along(grad_win[tok_rows - STRETCH :], "seq", 1)
    attended = jnp.concatenate([att_before[1:], att_win[: tok_rows - STRETCH + 1]])
    d_query = jnp.concatenate([grad_before[1:], grad_win[: tok_rows - STRETCH + 1]])

    raw_sum = lax.psum(lax.psum(bias_part, "seq"), "grp")
    squares = lax.psum(jnp.sum(raw_sum * raw_sum), "mp")
    d_bias = raw_sum * jnp.minimum(1.0, 1.0 / jnp.sqrt(squares + 1e-12))
    return (attended[None], d_query[None], d_kv[None], d_bias)


def solution(mesh):
    in_specs = (
        P("grp", "seq", "mp"),
        P("grp", "seq", "mp"),
        P("grp", "seq", None, None, "mp"),
        P("grp", "seq"),
        P("mp", None),
    )
    out_specs = (
        P("grp", "seq", "mp"),
        P("grp", "seq", "mp"),
        P("grp", "seq", None, None, "mp"),
        P("mp", None),
    )
    return jax.shard_map(local, mesh=mesh, in_specs=in_specs, out_specs=out_specs, check_vma=False)
```

time: 1040 us -> 432 us (0.42)
  waiting for transfers between devices: 522 us -> 147 us
  blocking collectives: 266 us -> 175 us
  starting transfers between devices: 77.1 us -> 24.9 us
  local copies, waits for them, and re-layouts: 90.5 us -> 44.1 us
  matrix products: 42.5 us -> 8.49 us
  between operations: 2.07 us -> 15 us
  other arithmetic: 25.1 us -> 12.3 us
    all_to_all x8 -> x2, waiting for transfers between devices: 352 us -> 5.28 us  [exchange(): return lax.all_to_all(block, 'seq', split_axis=0, concat_axis=0, tiled=True)]
    ppermute x3 -> x2, waiting for transfers between devices: 171 us -> 1.84 us  [passed_along(): return lax.ppermute(block, axis, route)]
    all_gather x0 -> x2, waiting for transfers between devices: none -> 139 us  [the longest x1 70.5 us: local(): g_all = lax.all_gather(d_out[0], 'seq', axis=0, tiled=True)]
    psum x1 -> x2, blocking collectives: 257 us -> 133 us  [local(): raw_sum = lax.psum(lax.psum(bias_part, 'seq'), 'grp')]
    all_to_all x8 -> x2, starting transfers between devices: 69.3 us -> 14.2 us  [exchange(): return lax.all_to_all(block, 'seq', split_axis=0, concat_axis=0, tiled=True)]
    unnamed x26 -> x29, local copies, waits for them, and re-layouts: 44.6 us -> 8.74 us
    dot_general x16 -> x1, matrix products: 36 us -> 0.85 us  [local(): jnp.einsum('sxihj,sxihd->sjxhd', mix_probs, mix_rows, preferred_element_t...]
    all_gather x0 -> x1, blocking collectives: none -> 32.1 us  [local(): shared_all = lax.all_gather(shared, 'seq', tiled=True)]
  transfers between devices with their start and end apart: 11 -> 7, of which waited for: 9 -> 4; matrix products, arithmetic and copies ran while one was open for 10% -> 11% of each run, Pallas kernels for 0% -> 0%
where the time goes in v1:
time: 432 us; the launch traced here: 427 us
  blocking collectives  175 us (41%)
  waiting for transfers between devices  147 us (34%)
  local copies, waits for them, and re-layouts  44.1 us (10%)
  starting transfers between devices  24.9 us (6%)
  between operations  15 us (3%)
  other arithmetic  12.3 us (3%)
  matrix products  8.49 us (2%)
    psum x2, blocking collectives, local(): raw_sum = lax.psum(lax.psum(bias_part, 'seq'), 'grp')  133 us
    all_gather x1, waiting for transfers between devices, local(): g_all = lax.all_gather(d_out[0], 'seq', axis=0, tiled=True)  70.5 us
    all_gather x1, waiting for transfers between devices, local(): q_all = lax.all_gather(queries[0], 'seq', axis=0, tiled=True)  68.3 us
    all_gather x1, blocking collectives, local(): shared_all = lax.all_gather(shared, 'seq', tiled=True)  32.1 us
    all_to_all x2, starting transfers between devices, exchange(): return lax.all_to_all(block, 'seq', split_axis=0, concat_axis=0, tiled=True)  14.2 us
    ppermute x2, starting transfers between devices, passed_along(): return lax.ppermute(block, axis, route)  10.5 us
    psum x1, blocking collectives, local(): squares = lax.psum(jnp.sum(raw_sum * raw_sum), 'mp')  9.79 us
    unnamed x29, local copies, waits for them, and re-layouts  8.74 us
  transfers between devices with their start and end apart: 7, of which 4 were waited for; matrix products, arithmetic and copies ran while one was open for 11% of the time, Pallas kernels for 0%

profile of v1, /device:TPU:1, one launch (start us, length us, event | category | flops | bytes accessed | tf_op | source)
XLA Modules:
  0.0 426.9 jit_solution(3914705341878619618)
XLA Ops:
  11.6 3.8 copy.83
  16.4 2.8 fusion.60
  19.2 70.5 %all-gather.7.cloned.1.call-done = bf16[1,4096,512]{2,1,0:T(8,128)(2,1)} async-done(((bf16[1,128,512]{2,1,0:T(8,128)(2,1)}), bf16[1,4096,512]{2,1,0:T(8,128)(2,1)}) %all-gather.7.cloned.1.call-update) | async-done | bytes 4194320 | tf_op jit(solution)/shard_map/all_gather | solution.py:62
  89.6 4.7 %gather_fusion.6 = bf16[512,512]{1,0:T(8,128)(2,1)S(1)} fusion(bf16[4096,512]{1,0:T(8,128)(2,1)} %bitcast.151, s32[1024]{0:T(1024)S(1)} %pad_clamp_fusion.3), kind=kCustom, calls=%fused_computation.1.clone | custom fusion | bytes 1050624 | tf_op jit(solution)/shard_map/jit(_take)/gather | solution.py:73
  94.4 68.3 %all-gather.5.cloned.1.call-done = bf16[1,4096,512]{2,1,0:T(8,128)(2,1)} async-done(((bf16[1,128,512]{2,1,0:T(8,128)(2,1)}), bf16[1,4096,512]{2,1,0:T(8,128)(2,1)}) %all-gather.5.cloned.1.call-update) | async-done | bytes 4194320 | tf_op jit(solution)/shard_map/all_gather | solution.py:61
  162.7 4.7 %gather_fusion.5 = bf16[512,512]{1,0:T(8,128)(2,1)S(1)} fusion(bf16[4096,512]{1,0:T(8,128)(2,1)} %bitcast.152, s32[1024]{0:T(1024)S(1)} %pad_clamp_fusion.3), kind=kCustom, calls=%fused_computation.clone | custom fusion | bytes 1050624 | tf_op jit(solution)/shard_map/jit(_take)/gather | solution.py:72
  167.6 1.0 reshape.666
  168.5 0.9 reshape.662
  169.4 1.7 fusion.62
  171.1 3.2 fusion.9
  174.8 32.1 %all_gather.11 = f32[256,769]{1,0:T(8,128)S(1)} all-gather(f32[8,769]{1,0:T(8,128)S(1)} %pad_maximum_fusion.3), channel_id=1, replica_groups=mesh['grp'=4,'seq'=32,'mp'=4] {'seq'}, dimensions={0}, use_global_device_ids=true | all-gather | bytes 812064 | tf_op jit(solution)/shard_map/all_gather | solution.py:144
  207.8 1.1 copy.142
  210.6 7.1 %all-to-all-start = ((f32[32,1,513]{2,1,0:T(1,128)}), f32[32,1,513]{2,1,0:T(1,128)S(1)}, u32[]{:S(2)}, u32[]{:S(2)}) async-start(f32[32,1,513]{2,1,0:T(1,128)} %copy.89), calls=%async_computation | async-start | bytes 163840 | tf_op jit(solution)/shard_map/all_to_all | solution.py:43
  217.7 2.0 gather_fusion.2
  219.7 3.3 select_select_fusion
  223.1 0.9 slice.114
  224.0 1.7 gather_fusion.4
  226.2 5.3 %all-to-all-done = f32[32,1,513]{2,1,0:T(1,128)S(1)} async-done(((f32[32,1,513]{2,1,0:T(1,128)}), f32[32,1,513]{2,1,0:T(1,128)S(1)}, u32[]{:S(2)}, u32[]{:S(2)}) %all-to-all-start) | async-done | bytes 65696 | tf_op jit(solution)/shard_map/all_to_all | solution.py:43
  231.4 7.1 %all-to-all-start.1 = ((bf16[32,64,512]{2,1,0:T(8,128)(2,1)}), bf16[32,64,512]{2,1,0:T(8,128)(2,1)}, u32[]{:S(2)}, u32[]{:S(2)}) async-start(bf16[32,64,512]{2,1,0:T(8,128)(2,1)} %select_select_fusion), calls=%async_computation.1 | async-start | bytes 4194304 | tf_op jit(solution)/shard_map/all_to_all | solution.py:43
  238.7 1.9 fusion.3
  241.7 2.4 broadcast_in_dim.191
  244.1 2.6 scatter_fusion
  247.9 0.9 fusion.61
  249.5 124.4 %psum.21 = f32[4,191]{1,0:T(4,128)S(1)} all-reduce(f32[4,191]{1,0:T(4,128)S(1)} %reduce_sum.58), channel_id=1, replica_groups=mesh['grp'=4,'seq'=32,'mp'=4] {'seq'}, use_global_device_ids=true, to_apply=%region_13.15 | all-reduce | flops 764 | bytes 6112 | tf_op jit(solution)/shard_map/psum | solution.py:184
  373.9 8.5 %psum.22 = f32[4,191]{1,0:T(4,128)S(1)} all-reduce(f32[4,191]{1,0:T(4,128)S(1)} %psum.21), channel_id=1, replica_groups=mesh['grp'=4,'seq'=32,'mp'=4] {'grp'}, use_global_device_ids=true, to_apply=%region_14.16 | all-reduce | flops 764 | bytes 6112 | tf_op jit(solution)/shard_map/psum | solution.py:184
  383.0 9.8 %psum.23 = f32[]{:T(128)} all-reduce(f32[]{:T(128)} %multiply_reduce_fusion.1), channel_id=1, replica_groups=mesh['grp'=4,'seq'=32,'mp'=4] {'mp'}, use_global_device_ids=true, to_apply=%region_16.18 | all-reduce | flops 1 | bytes 8 | tf_op jit(solution)/shard_map/psum | solution.py:185
  395.3 3.8 copy.108
  401.6 2.2 gather_fusion.3
  404.7 6.9 %collective-permute-start = (bf16[64,512]{1,0:T(8,128)(2,1)S(1)}, bf16[64,512]{1,0:T(8,128)(2,1)S(1)}, u32[]{:S(2)}, u32[]{:S(2)}) collective-permute-start(bf16[64,512]{1,0:T(8,128)(2,1)S(1)} %bitcast.173), channel_id=1, source_target_pairs={{0,4},{4,8},{8,12},{12,16},{16,20},{20,24},{24,28},{28,32},{32,36}... | collective-permute-start | bytes 196616 | tf_op jit(solution)/shard_map/ppermute | solution.py:14
  411.7 1.8 collective-permute-done
  414.5 3.6 collective-permute-start.1
  418.8 0.9 slice.120
  (127 shorter events, 19.8 us)
Async XLA Ops:
  7.2 4.4 %copy-start.6 = (bf16[1,8,128,2,512]{4,3,2,1,0:T(2,128)(2,1)S(1)}, bf16[1,8,128,2,512]{4,3,2,1,0:T(2,128)(2,1)}, u32[]{:S(2)}) copy-start(bf16[1,8,128,2,512]{4,3,2,1,0:T(2,128)(2,1)} %param.10) | copy-start | bytes 6291460
  7.2 82.5 %all-gather.7.cloned.1.call-start = ((), (), s32[]{:S(2)}) async-start(), calls=%async_computation.5 | async-start | bytes 4325376 | tf_op jit(solution)/shard_map/all_gather | solution.py:62
  7.9 154.7 %all-gather.5.cloned.1.call-start = ((), (), s32[]{:S(2)}) async-start(), calls=%async_computation.4 | async-start | bytes 4325376 | tf_op jit(solution)/shard_map/all_gather | solution.py:61
  11.6 3.8 copy-start.10
  167.5 3.6 copy-start.2
  169.4 1.7 copy-start.7
  206.9 0.9 copy-start.4
  210.6 20.8 %all-to-all-start = ((f32[32,1,513]{2,1,0:T(1,128)}), f32[32,1,513]{2,1,0:T(1,128)S(1)}, u32[]{:S(2)}, u32[]{:S(2)}) async-start(f32[32,1,513]{2,1,0:T(1,128)} %copy.89), calls=%async_computation | async-start | bytes 163840 | tf_op jit(solution)/shard_map/all_to_all | solution.py:43
  219.7 3.4 copy-start.5
  226.2 12.5 %copy-start.8 = (bf16[8,64,4,128]{3,2,1,0:T(4,128)(2,1)S(1)}, bf16[8,64,4,128]{3,2,1,0:T(4,128)(2,1)}, u32[]{:S(2)}) copy-start(bf16[8,64,4,128]{3,2,1,0:T(4,128)(2,1)} %reshape.666) | copy-start | bytes 1572868
  231.4 170.2 %all-to-all-start.1 = ((bf16[32,64,512]{2,1,0:T(8,128)(2,1)}), bf16[32,64,512]{2,1,0:T(8,128)(2,1)}, u32[]{:S(2)}, u32[]{:S(2)}) async-start(bf16[32,64,512]{2,1,0:T(8,128)(2,1)} %select_select_fusion), calls=%async_computation.1 | async-start | bytes 4194304 | tf_op jit(solution)/shard_map/all_to_all | solution.py:43
  238.6 175.1 %reduce-scatter.2.cloned.1.call-start = ((), (), s32[]{:S(2)}) async-start(), calls=%async_computation.3 | async-start | bytes 4325376 | tf_op jit(solution)/shard_map/reduce_scatter | solution.py:178
  240.6 1.0 copy-start
  246.7 1.2 copy-start.1
  246.7 146.1 %copy-start.3 = (bf16[512,512]{1,0:T(8,128)(2,1)S(1)}, bf16[512,512]{1,0:T(8,128)(2,1)}, u32[]{:S(2)}) copy-start(bf16[512,512]{1,0:T(8,128)(2,1)} %copy-done.2) | copy-start | bytes 1572868
  393.1 1.3 copy-start.9
  393.1 1.3 copy-start.11
  404.7 8.9 %collective-permute-start = (bf16[64,512]{1,0:T(8,128)(2,1)S(1)}, bf16[64,512]{1,0:T(8,128)(2,1)S(1)}, u32[]{:S(2)}, u32[]{:S(2)}) collective-permute-start(bf16[64,512]{1,0:T(8,128)(2,1)S(1)} %bitcast.173), channel_id=1, source_target_pairs={{0,4},{4,8},{8,12},{12,16},{16,20},{20,24},{24,28},{28,32},{32,36}... | collective-permute-start | bytes 196616 | tf_op jit(solution)/shard_map/ppermute | solution.py:14
  414.5 5.2 %collective-permute-start.1 = (bf16[64,512]{1,0:T(8,128)(2,1)S(1)}, bf16[64,512]{1,0:T(8,128)(2,1)S(1)}, u32[]{:S(2)}, u32[]{:S(2)}) collective-permute-start(bf16[64,512]{1,0:T(8,128)(2,1)S(1)} %slice_bitcast_fusion.1), channel_id=1, source_target_pairs={{0,4},{4,8},{8,12},{12,16},{16,20},{20,24},{24,28},{28,32},{32,36}... | collective-permute-start | bytes 196616 | tf_op jit(solution)/shard_map/ppermute | solution.py:14
Sparse Core Ops, SparseCore 0:
  10.1 79.4 all-gather.6
  91.8 70.8 all-gather.4
  246.8 152.4 reduce-scatter.1

commit v2 on v1

--- a/solution.py
+++ b/solution.py
@@ -58,8 +58,8 @@
     bias_rows = bias_grid(bias, STRETCH, NB_LEN).transpose(1, 0, 2)
     row_ids = jnp.arange(STRETCH)
 
-    q_all = lax.all_gather(queries[0], "seq", axis=0, tiled=True)
-    g_all = lax.all_gather(d_out[0], "seq", axis=0, tiled=True)
+    pair = jnp.stack([queries[0], d_out[0]], axis=1)
+    pair_all = lax.all_gather(pair, "seq", axis=0, tiled=True)
 
     my_targets = target[0]
     slot_count = my_targets.shape[0]
@@ -69,8 +69,9 @@
     win_rows = stretch_of[:, None] * STRETCH + (STRETCH - 1) + row_ids[None, :]
     in_group = win_rows < group_rows
     win_rows = jnp.minimum(win_rows.reshape(-1), group_rows - 1)
-    q_win = jnp.take(q_all, win_rows, axis=0).reshape(slot_count, STRETCH, width_dev)
-    g_win = jnp.take(g_all, win_rows, axis=0).reshape(slot_count, STRETCH, width_dev)
+    win = jnp.take(pair_all, win_rows, axis=0).reshape(slot_count, STRETCH, 2, width_dev)
+    q_win = win[:, :, 0]
+    g_win = win[:, :, 1]
     live_slot = (row_ids[None, :] == 0) | ((stretch_of[:, None] + 1) % seq_stretches != 0)
     q_keep = is_used[:, None] & in_group
     q_slots = jnp.where(q_keep[:, :, None], q_win, jnp.zeros((), q_win.dtype))
@@ -100,39 +101,6 @@
     part_send = take_rows(
         partial_value.astype(jnp.bfloat16).reshape(slot_count, STRETCH, width_dev), send_slot, send_has
     )
-    slot_stats = jnp.concatenate(
-        [
-            jnp.stack([peak_val, row_total], axis=1).reshape(slot_count, -1),
-            (entry + 1).astype(jnp.float32)[:, None],
-        ],
-        axis=1,
-    )
-    stat_send = take_rows(slot_stats, send_slot, send_has)
-    part_recv = exchange(part_send)
-    stat_recv = exchange(stat_send)
-
-    own_entries = my_index * per_owner + jnp.arange(per_owner)
-    sent_ids = stat_recv[:, -1].astype(jnp.int32) - 1
-    where_held = sent_ids[None, :] == own_entries[:, None]
-    held_by = jnp.argmax(where_held, axis=1)
-    parts_own = jnp.take(part_recv, held_by, axis=0).astype(jnp.float32)
-    parts_own = parts_own.reshape(stretch_count, 2, STRETCH, head_count, head_depth)
-    stats_own = jnp.take(stat_recv[:, :-1], held_by, axis=0)
-    stats_own = stats_own.reshape(stretch_count, 2, 2, STRETCH, head_count)
-    peaks_own = stats_own[:, :, 0]
-    totals_own = stats_own[:, :, 1]
-
-    stretch_ids = my_index * stretch_count + jnp.arange(stretch_count)
-    is_live = (row_ids[None, :] == 0) | ((stretch_ids[:, None] + 1) % seq_stretches != 0)
-    live_rows = is_live.astype(jnp.float32)
-    top_peak = jnp.max(peaks_own, axis=1)
-    factor = jnp.exp(peaks_own - top_peak[:, None])
-    denominator = jnp.sum(factor * totals_own, axis=1)
-    combined = jnp.sum(factor[..., None] * parts_own, axis=1) / denominator[..., None]
-    combined = combined * live_rows[:, :, None, None]
-    att_win = combined.astype(jnp.bfloat16).reshape(tok_rows, width_dev)
-    att_before = passed_along(att_win[tok_rows - STRETCH :], "seq", 1)
-
     g_dot = jnp.einsum(
         "sihd,sihd->sih", g_slots.astype(jnp.float32), partial_value, precision=lax.Precision.HIGHEST
     )
@@ -152,6 +120,29 @@
     lse_slots = both_peak + jnp.log(both_total)
     dd_slots = (mine_f * mine[:, 2] + theirs_f * theirs[:, 2]) / both_total
     dd_slots = jnp.where(is_used[:, None, None], dd_slots, 0.0)
+
+    part_recv = exchange(part_send)
+
+    own_entries = my_index * per_owner + jnp.arange(per_owner)
+    own_at = jnp.argmax(shared_all[None, :, -1] == (own_entries + 1).astype(jnp.float32)[:, None], axis=1)
+    held_by = own_at // slot_count
+    parts_own = jnp.take(part_recv, held_by, axis=0).astype(jnp.float32)
+    parts_own = parts_own.reshape(stretch_count, 2, STRETCH, head_count, head_depth)
+    stats_own = jnp.take(shared_all[:, :-1], own_at, axis=0).reshape(stretch_count, 2, 3, STRETCH, head_count)
+    peaks_own = stats_own[:, :, 0]
+    totals_own = stats_own[:, :, 1]
+
+    stretch_ids = my_index * stretch_count + jnp.arange(stretch_count)
+    is_live = (row_ids[None, :] == 0) | ((stretch_ids[:, None] + 1) % seq_stretches != 0)
+    live_rows = is_live.astype(jnp.float32)
+    top_peak = jnp.max(peaks_own, axis=1)
+    factor = jnp.exp(peaks_own - top_peak[:, None])
+    denominator = jnp.sum(factor * totals_own, axis=1)
+    combined = jnp.sum(factor[..., None] * parts_own, axis=1) / denominator[..., None]
+    combined = combined * live_rows[:, :, None, None]
+    att_win = combined.astype(jnp.bfloat16).reshape(tok_rows, width_dev)
+    att_before = passed_along(att_win[tok_rows - STRETCH :], "seq", 1)
+
     prob_full = jnp.exp(scores - lse_slots[..., None])
     prob_low = prob_full.astype(jnp.bfloat16)
     grad_prob = jnp.einsum(

time: 432 us -> 353 us (0.82)
  waiting for transfers between devices: 147 us -> 75.2 us
  starting transfers between devices: 24.9 us -> 17.8 us
  other arithmetic: 12.3 us -> 18.1 us
    all_gather x2 -> x1, waiting for transfers between devices: 139 us -> 73.3 us  [local(): pair_all = lax.all_gather(pair, 'seq', axis=0, tiled=True)]
    all_to_all x2 -> x1, starting transfers between devices: 14.2 us -> 7.14 us  [exchange(): return lax.all_to_all(block, 'seq', split_axis=0, concat_axis=0, tiled=True)]
    all_to_all x2 -> x1, waiting for transfers between devices: 5.28 us -> 0.01 us  [exchange(): return lax.all_to_all(block, 'seq', split_axis=0, concat_axis=0, tiled=True)]
    gather x4 -> x3, local copies, waits for them, and re-layouts: 10.2 us -> 8.53 us  [the longest x1 6.37 us: local(): jnp.take(pair_all, win_rows, axis=0)]
    unnamed x29 -> x66, local copies, waits for them, and re-layouts: 8.74 us -> 9.53 us
  transfers between devices with their start and end apart: 7 -> 5, of which waited for: 4 -> 2; matrix products, arithmetic and copies ran while one was open for 11% -> 10% of each run, Pallas kernels for 0% -> 0%
where the time goes in v2:
time: 353 us; the launch traced here: 349 us
  blocking collectives  175 us (50%)
  waiting for transfers between devices  75.2 us (21%)
  local copies, waits for them, and re-layouts  42.3 us (12%)
  other arithmetic  18.1 us (5%)
  starting transfers between devices  17.8 us (5%)
  between operations  15.4 us (4%)
  matrix products  4.95 us (1%)
    psum x2, blocking collectives, local(): raw_sum = lax.psum(lax.psum(bias_part, 'seq'), 'grp')  133 us
    all_gather x1, waiting for transfers between devices, local(): pair_all = lax.all_gather(pair, 'seq', axis=0, tiled=True)  73.3 us
    all_gather x1, blocking collectives, local(): shared_all = lax.all_gather(shared, 'seq', tiled=True)  32.1 us
    ppermute x2, starting transfers between devices, passed_along(): return lax.ppermute(block, axis, route)  10.5 us
    psum x1, blocking collectives, local(): squares = lax.psum(jnp.sum(raw_sum * raw_sum), 'mp')  9.59 us
    unnamed x66, local copies, waits for them, and re-layouts  9.53 us
    all_to_all x1, starting transfers between devices, exchange(): return lax.all_to_all(block, 'seq', split_axis=0, concat_axis=0, tiled=True)  7.14 us
  transfers between devices with their start and end apart: 5, of which 2 were waited for; matrix products, arithmetic and copies ran while one was open for 10% of the time, Pallas kernels for 0%

profile of v2, /device:TPU:1, one launch (start us, length us, event | category | flops | bytes accessed | tf_op | source)
XLA Modules:
  0.0 348.8 jit_solution(14778393523272404605)
XLA Ops:
  7.2 1.1 pad_maximum_fusion.1
  8.4 1.0 copy.104
  12.3 3.8 %copy.106 = bf16[1,8,128,2,512]{2,4,1,3,0:T(8,128)(2,1)} copy(bf16[1,8,128,2,512]{4,3,2,1,0:T(2,128)(2,1)S(1)} %copy-done.7) | data formatting | bytes 4194304 | tf_op args[2]
  19.4 2.8 fusion.54
  22.2 73.3 %all-gather.2.cloned.1.call-done = bf16[4096,2,512]{2,1,0:T(2,128)(2,1)} async-done(((bf16[128,2,512]{2,1,0:T(2,128)(2,1)}), bf16[4096,2,512]{2,1,0:T(2,128)(2,1)}) %all-gather.2.cloned.1.call-update) | async-done | bytes 8388624 | tf_op jit(solution)/shard_map/all_gather | solution.py:62
  95.4 6.4 %gather_fusion = bf16[512,2,512]{2,1,0:T(2,128)(2,1)S(1)} fusion(bf16[4096,2,512]{2,1,0:T(2,128)(2,1)} %all-gather.2.cloned.1.call-done, s32[1024]{0:T(1024)S(1)} %pad_clamp_fusion.4), kind=kCustom, calls=%fused_computation | custom fusion | bytes 2099200 | tf_op jit(solution)/shard_map/jit(_take)/gather | solution.py:72
  103.1 1.4 fusion.53
  105.1 2.0 multiply_reduce_fusion
  107.5 32.1 %all_gather.7 = f32[256,769]{1,0:T(8,128)S(1)} all-gather(f32[8,769]{1,0:T(8,128)S(1)} %pad_maximum_fusion.3), channel_id=1, replica_groups=mesh['grp'=4,'seq'=32,'mp'=4] {'seq'}, dimensions={0}, use_global_device_ids=true | all-gather | bytes 812064 | tf_op jit(solution)/shard_map/all_gather | solution.py:112
  139.7 0.9 slice.105
  142.0 2.3 gather_fusion.4
  144.3 0.9 copy.120
  146.0 2.3 gather_fusion.2
  148.3 3.3 select_select_fusion
  151.6 7.1 %all-to-all-start = ((bf16[32,64,512]{2,1,0:T(8,128)(2,1)}), bf16[32,64,512]{2,1,0:T(8,128)(2,1)}, u32[]{:S(2)}, u32[]{:S(2)}) async-start(bf16[32,64,512]{2,1,0:T(8,128)(2,1)} %select_select_fusion), calls=%async_computation | async-start | bytes 4194304 | tf_op jit(solution)/shard_map/all_to_all | solution.py:43
  159.8 1.0 copy-done
  160.7 0.8 fusion.5
  161.7 2.4 broadcast_in_dim.169
  164.1 2.6 scatter_fusion
  167.9 0.9 fusion.55
  169.4 124.6 %psum.21 = f32[4,191]{1,0:T(4,128)S(1)} all-reduce(f32[4,191]{1,0:T(4,128)S(1)} %reduce_sum.58), channel_id=1, replica_groups=mesh['grp'=4,'seq'=32,'mp'=4] {'seq'}, use_global_device_ids=true, to_apply=%region_13.14 | all-reduce | flops 764 | bytes 6112 | tf_op jit(solution)/shard_map/psum | solution.py:175
  294.1 8.9 %psum.22 = f32[4,191]{1,0:T(4,128)S(1)} all-reduce(f32[4,191]{1,0:T(4,128)S(1)} %psum.21), channel_id=1, replica_groups=mesh['grp'=4,'seq'=32,'mp'=4] {'grp'}, use_global_device_ids=true, to_apply=%region_14.15 | all-reduce | flops 764 | bytes 6112 | tf_op jit(solution)/shard_map/psum | solution.py:175
  303.5 9.6 %psum.23 = f32[]{:T(128)} all-reduce(f32[]{:T(128)} %multiply_reduce_fusion.2), channel_id=1, replica_groups=mesh['grp'=4,'seq'=32,'mp'=4] {'mp'}, use_global_device_ids=true, to_apply=%region_16.17 | all-reduce | flops 1 | bytes 8 | tf_op jit(solution)/shard_map/psum | solution.py:176
  314.3 1.8 gather_fusion.1
  317.8 0.9 multiply_convert_fusion
  318.6 3.8 %copy.129 = bf16[1,8,128,2,512]{4,3,2,1,0:T(2,128)(2,1)} copy(bf16[1,8,128,2,512]{2,4,3,1,0:T(8,128)(2,1)S(1)} %bitcast.165) | data formatting | bytes 4194304
  323.2 2.2 gather_fusion.3
  326.3 7.0 %collective-permute-start = (bf16[64,512]{1,0:T(8,128)(2,1)S(1)}, bf16[64,512]{1,0:T(8,128)(2,1)S(1)}, u32[]{:S(2)}, u32[]{:S(2)}) collective-permute-start(bf16[64,512]{1,0:T(8,128)(2,1)S(1)} %bitcast.180), channel_id=1, source_target_pairs={{0,4},{4,8},{8,12},{12,16},{16,20},{20,24},{24,28},{28,32},{32,36}... | collective-permute-start | bytes 196616 | tf_op jit(solution)/shard_map/ppermute | solution.py:14
  333.4 1.9 collective-permute-done
  335.3 0.8 slice_bitcast_fusion.1
  336.1 3.6 %collective-permute-start.1 = (bf16[64,512]{1,0:T(8,128)(2,1)S(1)}, bf16[64,512]{1,0:T(8,128)(2,1)S(1)}, u32[]{:S(2)}, u32[]{:S(2)}) collective-permute-start(bf16[64,512]{1,0:T(8,128)(2,1)S(1)} %slice_bitcast_fusion.1), channel_id=1, source_target_pairs={{0,4},{4,8},{8,12},{12,16},{16,20},{20,24},{24,28},{28,32},{32,36}... | collective-permute-start | bytes 196616 | tf_op jit(solution)/shard_map/ppermute | solution.py:14
  340.4 0.9 slice.118
  (155 shorter events, 19.3 us)
Async XLA Ops:
  7.2 5.1 %copy-start.7 = (bf16[1,8,128,2,512]{4,3,2,1,0:T(2,128)(2,1)S(1)}, bf16[1,8,128,2,512]{4,3,2,1,0:T(2,128)(2,1)}, u32[]{:S(2)}) copy-start(bf16[1,8,128,2,512]{4,3,2,1,0:T(2,128)(2,1)} %param.8) | copy-start | bytes 6291460
  7.2 88.3 %all-gather.2.cloned.1.call-start = ((), (), s32[]{:S(2)}) async-start(), calls=%async_computation.2 | async-start | bytes 8650752 | tf_op jit(solution)/shard_map/all_gather | solution.py:62
  10.0 8.6 %copy-start.22 = (pred[8]{0:T(512)(128)(4,1)}, pred[8]{0:T(512)(128)(4,1)S(1)}, u32[]{:S(2)}) copy-start(pred[8]{0:T(512)(128)(4,1)S(1)} %get-tuple-element.54) | copy-start | bytes 28
  12.3 3.8 %copy-start.24 = (s32[1,8]{1,0:T(1,128)S(1)}, s32[1,8]{1,0:T(1,128)}, u32[]{:S(2)}) copy-start(s32[1,8]{1,0:T(1,128)} %param.9) | copy-start | bytes 100
  16.1 6.1 %copy-start.25 = (pred[64]{0:T(512)(128)(4,1)}, pred[64]{0:T(512)(128)(4,1)S(1)}, u32[]{:S(2)}) copy-start(pred[64]{0:T(512)(128)(4,1)S(1)} %iota_compare_fusion.1) | copy-start | bytes 196
  18.7 83.7 %copy-start.18 = (pred[8,64]{1,0:T(8,128)(4,1)}, pred[8,64]{1,0:T(8,128)(4,1)S(1)}, u32[]{:S(2)}) copy-start(pred[8,64]{1,0:T(8,128)(4,1)S(1)} %get-tuple-element.51) | copy-start | bytes 1540
  18.7 84.4 %copy-start.16 = (pred[8,64]{1,0:T(8,128)(4,1)}, pred[8,64]{1,0:T(8,128)(4,1)S(1)}, u32[]{:S(2)}) copy-start(pred[8,64]{1,0:T(8,128)(4,1)S(1)} %get-tuple-element.50) | copy-start | bytes 1540
  102.1 2.5 copy-start.4
  102.4 2.2 copy-start.2
  107.1 34.8 %copy-start.11 = (f32[8,64,4]{1,2,0:T(4,128)}, f32[8,64,4]{1,2,0:T(4,128)S(1)}, u32[]{:S(2)}) copy-start(f32[8,64,4]{1,2,0:T(4,128)S(1)} %get-tuple-element.42) | copy-start | bytes 24580
  107.1 34.8 %copy-start.13 = (f32[8,64,4]{1,2,0:T(4,128)}, f32[8,64,4]{1,2,0:T(4,128)S(1)}, u32[]{:S(2)}) copy-start(f32[8,64,4]{1,2,0:T(4,128)S(1)} %get-tuple-element.59) | copy-start | bytes 24580
  107.5 34.4 %copy-start.6 = (bf16[8,4,8,8,128]{4,3,2,1,0:T(8,128)(2,1)S(1)}, bf16[8,4,8,8,128]{4,3,2,1,0:T(8,128)(2,1)}, u32[]{:S(2)}) copy-start(bf16[8,4,8,8,128]{4,3,2,1,0:T(8,128)(2,1)} %get-tuple-element.43) | copy-start | bytes 1572868
  139.7 2.2 copy-start.20
  146.0 2.3 copy-start.27
  146.0 2.3 copy-start.28
  151.5 7.2 %copy-start.10 = (f32[8,3,64,4]{2,3,0,1:T(4,128)S(1)}, f32[8,3,64,4]{2,3,0,1:T(4,128)}, u32[]{:S(2)}) copy-start(f32[8,3,64,4]{2,3,0,1:T(4,128)} %copy.121) | copy-start | bytes 73732
  151.5 7.2 %copy-start.29 = (pred[8]{0:T(512)(128)(4,1)S(1)}, pred[8]{0:T(512)(128)(4,1)}, u32[]{:S(2)}) copy-start(pred[8]{0:T(512)(128)(4,1)} %compare_and_fusion.1) | copy-start | bytes 28
  151.5 7.3 %copy-start.12 = (f32[8,64,4]{1,2,0:T(4,128)S(1)}, f32[8,64,4]{1,2,0:T(4,128)}, u32[]{:S(2)}) copy-start(f32[8,64,4]{1,2,0:T(4,128)} %copy-done.11) | copy-start | bytes 24580
  151.5 7.3 %copy-start.14 = (f32[8,64,4]{1,2,0:T(4,128)S(1)}, f32[8,64,4]{1,2,0:T(4,128)}, u32[]{:S(2)}) copy-start(f32[8,64,4]{1,2,0:T(4,128)} %copy-done.13) | copy-start | bytes 24580
  151.5 7.3 %copy-start.23 = (pred[8]{0:T(512)(128)(4,1)S(1)}, pred[8]{0:T(512)(128)(4,1)}, u32[]{:S(2)}) copy-start(pred[8]{0:T(512)(128)(4,1)} %copy-done.22) | copy-start | bytes 28
  151.6 7.4 %copy-start.8 = (bf16[8,64,4,128]{3,2,1,0:T(4,128)(2,1)S(1)}, bf16[8,64,4,128]{3,2,1,0:T(4,128)(2,1)}, u32[]{:S(2)}) copy-start(bf16[8,64,4,128]{3,2,1,0:T(4,128)(2,1)} %get-tuple-element.35) | copy-start | bytes 1572868
  151.6 171.6 %all-to-all-start = ((bf16[32,64,512]{2,1,0:T(8,128)(2,1)}), bf16[32,64,512]{2,1,0:T(8,128)(2,1)}, u32[]{:S(2)}, u32[]{:S(2)}) async-start(bf16[32,64,512]{2,1,0:T(8,128)(2,1)} %select_select_fusion), calls=%async_computation | async-start | bytes 4194304 | tf_op jit(solution)/shard_map/all_to_all | solution.py:43
  158.7 176.5 %reduce-scatter.2.cloned.1.call-start = ((), (), s32[]{:S(2)}) async-start(), calls=%async_computation.3 | async-start | bytes 4325376 | tf_op jit(solution)/shard_map/reduce_scatter | solution.py:169
  161.6 2.4 copy-start.15
  166.7 146.4 %copy-start.5 = (bf16[8,64,1,512]{3,1,0,2:T(8,128)(2,1)S(1)}, bf16[8,64,1,512]{3,1,0,2:T(8,128)(2,1)}, u32[]{:S(2)}) copy-start(bf16[8,64,1,512]{3,1,0,2:T(8,128)(2,1)} %copy-done.4) | copy-start | bytes 1572868
  168.8 144.6 %copy-start.21 = (f32[256]{0:T(256)S(1)}, f32[256]{0:T(256)}, u32[]{:S(2)}) copy-start(f32[256]{0:T(256)} %copy-done.20) | copy-start | bytes 3076
  313.1 4.4 %copy-start.17 = (pred[8,64]{1,0:T(8,128)(4,1)S(1)}, pred[8,64]{1,0:T(8,128)(4,1)}, u32[]{:S(2)}) copy-start(pred[8,64]{1,0:T(8,128)(4,1)} %copy-done.16) | copy-start | bytes 1540
  313.1 4.4 %copy-start.19 = (pred[8,64]{1,0:T(8,128)(4,1)S(1)}, pred[8,64]{1,0:T(8,128)(4,1)}, u32[]{:S(2)}) copy-start(pred[8,64]{1,0:T(8,128)(4,1)} %copy-done.18) | copy-start | bytes 1540
  314.3 3.5 copy-start.9
  314.3 3.5 copy-start.30
  326.3 8.9 %collective-permute-start = (bf16[64,512]{1,0:T(8,128)(2,1)S(1)}, bf16[64,512]{1,0:T(8,128)(2,1)S(1)}, u32[]{:S(2)}, u32[]{:S(2)}) collective-permute-start(bf16[64,512]{1,0:T(8,128)(2,1)S(1)} %bitcast.180), channel_id=1, source_target_pairs={{0,4},{4,8},{8,12},{12,16},{16,20},{20,24},{24,28},{28,32},{32,36}... | collective-permute-start | bytes 196616 | tf_op jit(solution)/shard_map/ppermute | solution.py:14
  336.1 5.2 %collective-permute-start.1 = (bf16[64,512]{1,0:T(8,128)(2,1)S(1)}, bf16[64,512]{1,0:T(8,128)(2,1)S(1)}, u32[]{:S(2)}, u32[]{:S(2)}) collective-permute-start(bf16[64,512]{1,0:T(8,128)(2,1)S(1)} %slice_bitcast_fusion.1), channel_id=1, source_target_pairs={{0,4},{4,8},{8,12},{12,16},{16,20},{20,24},{24,28},{28,32},{32,36}... | collective-permute-start | bytes 196616 | tf_op jit(solution)/shard_map/ppermute | solution.py:14
  (4 other events, 4.8 us)
Sparse Core Ops, SparseCore 0:
  10.1 85.2 all-gather.1
  166.8 152.6 reduce-scatter.1

commit v3 on v2

--- a/solution.py
+++ b/solution.py
@@ -109,7 +109,8 @@
         [mine.reshape(slot_count, -1), jnp.where(is_used, entry + 1, 0).astype(jnp.float32)[:, None]],
         axis=1,
     )
-    shared_all = lax.all_gather(shared, "seq", tiled=True)
+    shared_wide = jnp.pad(shared, ((0, 0), (0, 1024 - shared.shape[1])))
+    shared_all = lax.all_gather(shared_wide, "seq", tiled=True)[:, : shared.shape[1]]
     partner = entry + 1 - 2 * (entry % 2)
     partner_at = jnp.argmax(shared_all[None, :, -1] == (partner + 1).astype(jnp.float32)[:, None], axis=1)
     theirs = jnp.take(shared_all[:, :-1], partner_at, axis=0).reshape(mine.shape)

time: 353 us -> 343 us (0.972)
  blocking collectives: 175 us -> 64.1 us
  waiting for transfers between devices: 75.2 us -> 173 us
  local copies, waits for them, and re-layouts: 42.3 us -> 47.5 us
    psum x2, blocking collectives: 133 us -> 53.9 us  [local(): raw_sum = lax.psum(lax.psum(bias_part, 'seq'), 'grp')]
    all_gather x0 -> x1, waiting for transfers between devices: none -> 76.4 us  [local(): lax.all_gather(shared_wide, 'seq', tiled=True)[:, :shared.shape[1]]]
    all_gather x1 -> x0, blocking collectives: 32.1 us -> none  [local(): shared_all = lax.all_gather(shared, 'seq', tiled=True)]
    reduce_scatter x1, waiting for transfers between devices: 0.02 us -> 18.3 us  [local(): grad_win = lax.psum_scatter(dq_rows, 'seq', scatter_dimension=0, tiled=True)]
    unnamed x66 -> x58, local copies, waits for them, and re-layouts: 9.53 us -> 9.33 us
  transfers between devices with their start and end apart: 5 -> 6, of which waited for: 2 -> 5; matrix products, arithmetic and copies ran while one was open for 10% -> 16% of each run, Pallas kernels for 0% -> 0%
where the time goes in v3:
time: 343 us; the launch traced here: 342 us
  waiting for transfers between devices  173 us (50%)
  blocking collectives  64.1 us (19%)
  local copies, waits for them, and re-layouts  47.5 us (14%)
  other arithmetic  19.6 us (6%)
  starting transfers between devices  16.4 us (5%)
  between operations  15 us (4%)
  matrix products  6.32 us (2%)
    all_gather x1, waiting for transfers between devices, local(): lax.all_gather(shared_wide, 'seq', tiled=True)[:, :shared.shape[1]]  76.4 us
    all_gather x1, waiting for transfers between devices, local(): pair_all = lax.all_gather(pair, 'seq', axis=0, tiled=True)  75.7 us
    psum x2, blocking collectives, local(): raw_sum = lax.psum(lax.psum(bias_part, 'seq'), 'grp')  53.9 us
    reduce_scatter x1, waiting for transfers between devices, local(): grad_win = lax.psum_scatter(dq_rows, 'seq', scatter_dimension=0, tiled=True)  18.3 us
    psum x1, blocking collectives, local(): squares = lax.psum(jnp.sum(raw_sum * raw_sum), 'mp')  10.2 us
    unnamed x58, local copies, waits for them, and re-layouts  9.33 us
    ppermute x2, starting transfers between devices, passed_along(): return lax.ppermute(block, axis, route)  8.44 us
    all_to_all x1, starting transfers between devices, exchange(): return lax.all_to_all(block, 'seq', split_axis=0, concat_axis=0, tiled=True)  7.84 us
  transfers between devices with their start and end apart: 6, of which 5 were waited for; matrix products, arithmetic and copies ran while one was open for 16% of the time, Pallas kernels for 0%

profile of v3, /device:TPU:1, one launch (start us, length us, event | category | flops | bytes accessed | tf_op | source)
XLA Modules:
  0.0 341.9 jit_solution(12824938684409181369)
XLA Ops:
  7.2 1.1 pad_maximum_fusion.1
  8.4 1.0 copy.104
  12.3 3.8 %copy.106 = bf16[1,8,128,2,512]{2,4,1,3,0:T(8,128)(2,1)} copy(bf16[1,8,128,2,512]{4,3,2,1,0:T(2,128)(2,1)S(1)} %copy-done.8) | data formatting | bytes 4194304 | tf_op args[2]
  16.9 2.8 fusion.54
  19.7 75.7 %all-gather.3.cloned.1.call-done = bf16[4096,2,512]{2,1,0:T(2,128)(2,1)} async-done(((bf16[128,2,512]{2,1,0:T(2,128)(2,1)}), bf16[4096,2,512]{2,1,0:T(2,128)(2,1)}) %all-gather.3.cloned.1.call-update) | async-done | bytes 8388624 | tf_op jit(solution)/shard_map/all_gather | solution.py:62
  95.4 6.4 %gather_fusion = bf16[512,2,512]{2,1,0:T(2,128)(2,1)S(1)} fusion(bf16[4096,2,512]{2,1,0:T(2,128)(2,1)} %all-gather.3.cloned.1.call-done, s32[1024]{0:T(1024)S(1)} %pad_clamp_fusion.4), kind=kCustom, calls=%fused_computation | custom fusion | bytes 2099200 | tf_op jit(solution)/shard_map/jit(_take)/gather | solution.py:72
  103.1 1.4 fusion.53
  105.1 2.0 multiply_reduce_fusion
  108.9 1.1 copy.160
  110.1 2.0 gather_fusion.2
  112.1 3.3 select_select_fusion
  115.3 7.8 %all-to-all-start = ((bf16[32,64,512]{2,1,0:T(8,128)(2,1)}), bf16[32,64,512]{2,1,0:T(8,128)(2,1)}, u32[]{:S(2)}, u32[]{:S(2)}) async-start(bf16[32,64,512]{2,1,0:T(8,128)(2,1)} %select_select_fusion), calls=%async_computation | async-start | bytes 4194304 | tf_op jit(solution)/shard_map/all_to_all | solution.py:43
  123.2 76.4 %all-gather.5.cloned.1.call-done = f32[256,1024]{1,0:T(8,128)} async-done(((f32[8,1024]{1,0:T(8,128)}), f32[256,1024]{1,0:T(8,128)}) %all-gather.5.cloned.1.call-update) | async-done | bytes 1048592 | tf_op jit(solution)/shard_map/all_gather | solution.py:113
  199.6 1.0 slice_reduce_fusion
  201.9 2.1 slice.108
  203.9 2.3 gather_fusion.4
  212.4 2.4 broadcast_in_dim.169
  214.9 2.6 scatter_fusion
  219.4 1.0 squeeze.44
  220.4 1.0 fusion.55
  222.0 45.4 %psum.21 = f32[4,191]{1,0:T(4,128)S(1)} all-reduce(f32[4,191]{1,0:T(4,128)S(1)} %reduce_sum.58), channel_id=1, replica_groups=mesh['grp'=4,'seq'=32,'mp'=4] {'seq'}, use_global_device_ids=true, to_apply=%region_13.14 | all-reduce | flops 764 | bytes 6112 | tf_op jit(solution)/shard_map/psum | solution.py:176
  267.5 8.5 %psum.22 = f32[4,191]{1,0:T(4,128)S(1)} all-reduce(f32[4,191]{1,0:T(4,128)S(1)} %psum.21), channel_id=1, replica_groups=mesh['grp'=4,'seq'=32,'mp'=4] {'grp'}, use_global_device_ids=true, to_apply=%region_14.15 | all-reduce | flops 764 | bytes 6112 | tf_op jit(solution)/shard_map/psum | solution.py:176
  276.6 1.2 copy_select_fusion.1
  277.8 10.2 %psum.23 = f32[]{:T(128)} all-reduce(f32[]{:T(128)} %multiply_reduce_fusion.2), channel_id=1, replica_groups=mesh['grp'=4,'seq'=32,'mp'=4] {'mp'}, use_global_device_ids=true, to_apply=%region_16.17 | all-reduce | flops 1 | bytes 8 | tf_op jit(solution)/shard_map/psum | solution.py:177
  289.9 1.7 gather_fusion.1
  293.0 2.2 multiply_convert_fusion
  295.3 3.8 %copy.129 = bf16[1,8,128,2,512]{4,3,2,1,0:T(2,128)(2,1)} copy(bf16[1,8,128,2,512]{2,4,3,1,0:T(8,128)(2,1)S(1)} %bitcast.165) | data formatting | bytes 4194304
  299.9 2.2 gather_fusion.3
  302.9 5.1 %collective-permute-start = (bf16[64,512]{1,0:T(8,128)(2,1)S(1)}, bf16[64,512]{1,0:T(8,128)(2,1)S(1)}, u32[]{:S(2)}, u32[]{:S(2)}) collective-permute-start(bf16[64,512]{1,0:T(8,128)(2,1)S(1)} %bitcast.180), channel_id=1, source_target_pairs={{0,4},{4,8},{8,12},{12,16},{16,20},{20,24},{24,28},{28,32},{32,36}... | collective-permute-start | bytes 196616 | tf_op jit(solution)/shard_map/ppermute | solution.py:14
  308.2 1.8 collective-permute-done
  310.0 18.3 %reduce-scatter.2.cloned.1.call-done = bf16[1,2,64,512]{3,2,1,0:T(8,128)(2,1)} async-done(((bf16[32,2,64,512]{3,2,1,0:T(8,128)(2,1)}), bf16[1,2,64,512]{3,2,1,0:T(8,128)(2,1)}) %reduce-scatter.2.cloned.1.call-update) | async-done | bytes 131088 | tf_op jit(solution)/shard_map/reduce_scatter | solution.py:170
  329.2 3.3 collective-permute-start.1
  (149 shorter events, 25.9 us)
Async XLA Ops:
  7.2 5.2 %copy-start.8 = (bf16[1,8,128,2,512]{4,3,2,1,0:T(2,128)(2,1)S(1)}, bf16[1,8,128,2,512]{4,3,2,1,0:T(2,128)(2,1)}, u32[]{:S(2)}) copy-start(bf16[1,8,128,2,512]{4,3,2,1,0:T(2,128)(2,1)} %param.8) | copy-start | bytes 6291460
  7.2 88.3 %all-gather.3.cloned.1.call-start = ((), (), s32[]{:S(2)}) async-start(), calls=%async_computation.2 | async-start | bytes 8650752 | tf_op jit(solution)/shard_map/all_gather | solution.py:62
  9.4 190.3 %all-gather.5.cloned.1.call-start = ((), (), s32[]{:S(2)}) async-start(), calls=%async_computation.3 | async-start | bytes 1081344 | tf_op jit(solution)/shard_map/all_gather | solution.py:113
  10.1 6.1 %copy-start.21 = (pred[8]{0:T(512)(128)(4,1)}, pred[8]{0:T(512)(128)(4,1)S(1)}, u32[]{:S(2)}) copy-start(pred[8]{0:T(512)(128)(4,1)S(1)} %get-tuple-element.54) | copy-start | bytes 28
  16.1 3.6 %copy-start.23 = (pred[64]{0:T(512)(128)(4,1)}, pred[64]{0:T(512)(128)(4,1)S(1)}, u32[]{:S(2)}) copy-start(pred[64]{0:T(512)(128)(4,1)S(1)} %iota_compare_fusion.2) | copy-start | bytes 196
  16.2 86.1 %copy-start.17 = (pred[8,64]{1,0:T(8,128)(4,1)}, pred[8,64]{1,0:T(8,128)(4,1)S(1)}, u32[]{:S(2)}) copy-start(pred[8,64]{1,0:T(8,128)(4,1)S(1)} %get-tuple-element.51) | copy-start | bytes 1540
  16.2 86.9 %copy-start.15 = (pred[8,64]{1,0:T(8,128)(4,1)}, pred[8,64]{1,0:T(8,128)(4,1)S(1)}, u32[]{:S(2)}) copy-start(pred[8,64]{1,0:T(8,128)(4,1)S(1)} %get-tuple-element.50) | copy-start | bytes 1540
  102.1 2.5 copy-start.4
  102.4 2.2 copy-start.2
  105.1 3.1 copy-start.22
  107.1 1.8 copy-start.12
  107.1 1.8 copy-start.13
  115.3 184.5 %all-to-all-start = ((bf16[32,64,512]{2,1,0:T(8,128)(2,1)}), bf16[32,64,512]{2,1,0:T(8,128)(2,1)}, u32[]{:S(2)}, u32[]{:S(2)}) async-start(bf16[32,64,512]{2,1,0:T(8,128)(2,1)} %select_select_fusion), calls=%async_computation | async-start | bytes 4194304 | tf_op jit(solution)/shard_map/all_to_all | solution.py:43
  123.2 86.5 %copy-start.9 = (bf16[8,64,4,128]{3,2,1,0:T(4,128)(2,1)S(1)}, bf16[8,64,4,128]{3,2,1,0:T(4,128)(2,1)}, u32[]{:S(2)}) copy-start(bf16[8,64,4,128]{3,2,1,0:T(4,128)(2,1)} %get-tuple-element.35) | copy-start | bytes 1572868
  123.2 205.1 %reduce-scatter.2.cloned.1.call-start = ((), (), s32[]{:S(2)}) async-start(), calls=%async_computation.4 | async-start | bytes 4325376 | tf_op jit(solution)/shard_map/reduce_scatter | solution.py:170
  200.6 3.3 copy-start.19
  207.9 3.5 %copy-start.3 = (bf16[8,128,1,512]{1,3,0,2:T(8,128)(2,1)S(1)}, bf16[8,128,1,512]{1,3,0,2:T(8,128)(2,1)}, u32[]{:S(2)}) copy-start(bf16[8,128,1,512]{1,3,0,2:T(8,128)(2,1)} %get-tuple-element.38) | copy-start | bytes 3145732
  209.7 2.6 copy-start.10
  210.5 1.0 copy-start
  212.4 2.4 copy-start.14
  217.4 1.0 copy-start.5
  217.5 3.0 copy-start.1
  219.4 57.2 %copy-start.6 = (bf16[8,1,64,4,128]{4,3,2,0,1:T(4,128)(2,1)S(1)}, bf16[8,1,64,4,128]{4,3,2,0,1:T(4,128)(2,1)}, u32[]{:S(2)}) copy-start(bf16[8,1,64,4,128]{4,3,2,0,1:T(4,128)(2,1)} %squeeze.45) | copy-start | bytes 1572868
  219.4 57.2 %copy-start.16 = (pred[8,64]{1,0:T(8,128)(4,1)S(1)}, pred[8,64]{1,0:T(8,128)(4,1)}, u32[]{:S(2)}) copy-start(pred[8,64]{1,0:T(8,128)(4,1)} %copy-done.15) | copy-start | bytes 1540
  219.4 57.2 %copy-start.18 = (pred[8,64]{1,0:T(8,128)(4,1)S(1)}, pred[8,64]{1,0:T(8,128)(4,1)}, u32[]{:S(2)}) copy-start(pred[8,64]{1,0:T(8,128)(4,1)} %copy-done.17) | copy-start | bytes 1540
  220.4 56.2 %copy-start.7 = (bf16[8,1,64,4,128]{4,3,2,0,1:T(4,128)(2,1)S(1)}, bf16[8,1,64,4,128]{4,3,2,0,1:T(4,128)(2,1)}, u32[]{:S(2)}) copy-start(bf16[8,1,64,4,128]{4,3,2,0,1:T(4,128)(2,1)} %squeeze.44) | copy-start | bytes 1572868
  221.4 66.6 %copy-start.20 = (f32[256]{0:T(256)S(1)}, f32[256]{0:T(256)}, u32[]{:S(2)}) copy-start(f32[256]{0:T(256)} %copy-done.19) | copy-start | bytes 3076
  221.5 71.2 %copy-start.11 = (f32[8,64,4]{1,2,0:T(4,128)S(1)}, f32[8,64,4]{1,2,0:T(4,128)}, u32[]{:S(2)}) copy-start(f32[8,64,4]{1,2,0:T(4,128)} %copy-done.10) | copy-start | bytes 24580
  295.3 3.8 %copy-start.26 = (pred[2,2]{1,0:T(4,128)(4,1)S(1)}, pred[2,2]{1,0:T(4,128)(4,1)}, u32[]{:S(2)}) copy-start(pred[2,2]{1,0:T(4,128)(4,1)} %broadcast_in_dim.155) | copy-start | bytes 16
  299.1 3.0 copy-start.25
  302.9 7.1 %collective-permute-start = (bf16[64,512]{1,0:T(8,128)(2,1)S(1)}, bf16[64,512]{1,0:T(8,128)(2,1)S(1)}, u32[]{:S(2)}, u32[]{:S(2)}) collective-permute-start(bf16[64,512]{1,0:T(8,128)(2,1)S(1)} %bitcast.180), channel_id=1, source_target_pairs={{0,4},{4,8},{8,12},{12,16},{16,20},{20,24},{24,28},{28,32},{32,36}... | collective-permute-start | bytes 196616 | tf_op jit(solution)/shard_map/ppermute | solution.py:14
  329.2 5.5 %collective-permute-start.1 = (bf16[64,512]{1,0:T(8,128)(2,1)S(1)}, bf16[64,512]{1,0:T(8,128)(2,1)S(1)}, u32[]{:S(2)}, u32[]{:S(2)}) collective-permute-start(bf16[64,512]{1,0:T(8,128)(2,1)S(1)} %slice_bitcast_fusion.1), channel_id=1, source_target_pairs={{0,4},{4,8},{8,12},{12,16},{16,20},{20,24},{24,28},{28,32},{32,36}... | collective-permute-start | bytes 196616 | tf_op jit(solution)/shard_map/ppermute | solution.py:14
  (1 other events, 0.7 us)
Sparse Core Ops, SparseCore 0:
  10.1 85.2 all-gather.2
  108.3 91.2 all-gather.4
  217.6 110.7 reduce-scatter.1

commit v4 on v3

--- a/solution.py
+++ b/solution.py
@@ -122,6 +122,7 @@
     dd_slots = (mine_f * mine[:, 2] + theirs_f * theirs[:, 2]) / both_total
     dd_slots = jnp.where(is_used[:, None, None], dd_slots, 0.0)
 
+    part_send, shared_all = lax.optimization_barrier((part_send, shared_all))
     part_recv = exchange(part_send)
 
     own_entries = my_index * per_owner + jnp.arange(per_owner)

time: 343 us -> 390 us (1.14)
  blocking collectives: 64.1 us -> 141 us
  waiting for transfers between devices: 173 us -> 138 us
    psum x2, blocking collectives: 53.9 us -> 132 us  [local(): raw_sum = lax.psum(lax.psum(bias_part, 'seq'), 'grp')]
    reduce_scatter x1, waiting for transfers between devices: 18.3 us -> 0.02 us  [local(): grad_win = lax.psum_scatter(dq_rows, 'seq', scatter_dimension=0, tiled=True)]
    all_gather x1, waiting for transfers between devices: 76.4 us -> 60.2 us  [local(): lax.all_gather(shared_wide, 'seq', tiled=True)[:, :shared.shape[1]]]
    unnamed x58 -> x30, local copies, waits for them, and re-layouts: 9.33 us -> 11.7 us
  transfers between devices with their start and end apart: 6 -> 6, of which waited for: 5 -> 3; matrix products, arithmetic and copies ran while one was open for 16% -> 12% of each run, Pallas kernels for 0% -> 0%
where the time goes in v4:
time: 390 us; the launch traced here: 386 us
  blocking collectives  141 us (36%)
  waiting for transfers between devices  138 us (35%)
  local copies, waits for them, and re-layouts  48.1 us (12%)
  starting transfers between devices  19.8 us (5%)
  other arithmetic  15.9 us (4%)
  between operations  14.9 us (4%)
  matrix products  7.38 us (2%)
    psum x2, blocking collectives, local(): raw_sum = lax.psum(lax.psum(bias_part, 'seq'), 'grp')  132 us
    all_gather x1, waiting for transfers between devices, local(): pair_all = lax.all_gather(pair, 'seq', axis=0, tiled=True)  76.3 us
    all_gather x1, waiting for transfers between devices, local(): lax.all_gather(shared_wide, 'seq', tiled=True)[:, :shared.shape[1]]  60.2 us
    unnamed x30, local copies, waits for them, and re-layouts  11.7 us
    ppermute x2, starting transfers between devices, passed_along(): return lax.ppermute(block, axis, route)  11.1 us
    psum x1, blocking collectives, local(): squares = lax.psum(jnp.sum(raw_sum * raw_sum), 'mp')  9.58 us
    all_to_all x1, starting transfers between devices, exchange(): return lax.all_to_all(block, 'seq', split_axis=0, concat_axis=0, tiled=True)  8.61 us
  transfers between devices with their start and end apart: 6, of which 3 were waited for; matrix products, arithmetic and copies ran while one was open for 12% of the time, Pallas kernels for 0%

profile of v4, /device:TPU:1, one launch (start us, length us, event | category | flops | bytes accessed | tf_op | source)
XLA Modules:
  0.0 385.8 jit_solution(11728707167402899339)
XLA Ops:
  7.2 1.1 pad_maximum_fusion.1
  8.4 1.0 copy.104
  12.3 3.8 copy.106
  16.4 2.8 fusion.54
  19.2 76.3 %all-gather.3.cloned.1.call-done = bf16[4096,2,512]{2,1,0:T(2,128)(2,1)} async-done(((bf16[128,2,512]{2,1,0:T(2,128)(2,1)}), bf16[4096,2,512]{2,1,0:T(2,128)(2,1)}) %all-gather.3.cloned.1.call-update) | async-done | bytes 8388624 | tf_op jit(solution)/shard_map/all_gather | solution.py:62
  95.4 6.4 %gather_fusion = bf16[512,2,512]{2,1,0:T(2,128)(2,1)S(1)} fusion(bf16[4096,2,512]{2,1,0:T(2,128)(2,1)} %all-gather.3.cloned.1.call-done, s32[1024]{0:T(1024)S(1)} %pad_clamp_fusion.4), kind=kCustom, calls=%fused_computation | custom fusion | bytes 2099200 | tf_op jit(solution)/shard_map/jit(_take)/gather | solution.py:72
  103.1 1.4 fusion.53
  105.1 2.0 multiply_reduce_fusion
  108.9 1.1 copy.160
  110.0 2.0 gather_fusion.1
  112.0 3.3 select_select_fusion
  115.3 60.2 %all-gather.5.cloned.1.call-done = f32[256,1024]{1,0:T(8,128)} async-done(((f32[8,1024]{1,0:T(8,128)}), f32[256,1024]{1,0:T(8,128)}) %all-gather.5.cloned.1.call-update) | async-done | bytes 1048592 | tf_op jit(solution)/shard_map/all_gather | solution.py:113
  175.4 1.0 slice_reduce_fusion
  177.2 2.1 slice.125
  179.2 1.7 gather_fusion.4
  181.3 2.2 slice.116
  183.5 8.6 %all-to-all-start = ((bf16[32,64,512]{2,1,0:T(8,128)(2,1)}), bf16[32,64,512]{2,1,0:T(8,128)(2,1)}, u32[]{:S(2)}, u32[]{:S(2)}) async-start(bf16[32,64,512]{2,1,0:T(8,128)(2,1)} %select_select_fusion), calls=%async_computation | async-start | bytes 4194304 | tf_op jit(solution)/shard_map/all_to_all | solution.py:43
  193.1 1.0 copy-done
  195.0 2.4 broadcast_in_dim.169
  197.4 2.5 scatter_fusion
  200.9 1.0 squeeze.45
  201.9 1.0 squeeze.44
  202.9 0.9 fusion.55
  204.5 122.6 %psum.21 = f32[4,191]{1,0:T(4,128)S(1)} all-reduce(f32[4,191]{1,0:T(4,128)S(1)} %reduce_sum.58), channel_id=1, replica_groups=mesh['grp'=4,'seq'=32,'mp'=4] {'seq'}, use_global_device_ids=true, to_apply=%region_13.14 | all-reduce | flops 764 | bytes 6112 | tf_op jit(solution)/shard_map/psum | solution.py:177
  327.1 9.0 %psum.22 = f32[4,191]{1,0:T(4,128)S(1)} all-reduce(f32[4,191]{1,0:T(4,128)S(1)} %psum.21), channel_id=1, replica_groups=mesh['grp'=4,'seq'=32,'mp'=4] {'grp'}, use_global_device_ids=true, to_apply=%region_14.15 | all-reduce | flops 764 | bytes 6112 | tf_op jit(solution)/shard_map/psum | solution.py:177
  336.9 9.6 %psum.23 = f32[]{:T(128)} all-reduce(f32[]{:T(128)} %multiply_reduce_fusion.2), channel_id=1, replica_groups=mesh['grp'=4,'seq'=32,'mp'=4] {'mp'}, use_global_device_ids=true, to_apply=%region_16.17 | all-reduce | flops 1 | bytes 8 | tf_op jit(solution)/shard_map/psum | solution.py:178
  347.6 3.3 multiply_convert_fusion
  350.9 6.3 %copy.129 = bf16[1,8,128,2,512]{4,3,2,1,0:T(2,128)(2,1)} copy(bf16[1,8,128,2,512]{2,4,3,1,0:T(8,128)(2,1)} %bitcast.165) | data formatting | bytes 4194304
  359.9 2.2 gather_fusion.3
  363.0 7.5 %collective-permute-start = (bf16[64,512]{1,0:T(8,128)(2,1)S(1)}, bf16[64,512]{1,0:T(8,128)(2,1)S(1)}, u32[]{:S(2)}, u32[]{:S(2)}) collective-permute-start(bf16[64,512]{1,0:T(8,128)(2,1)S(1)} %bitcast.180), channel_id=1, source_target_pairs={{0,4},{4,8},{8,12},{12,16},{16,20},{20,24},{24,28},{28,32},{32,36}... | collective-permute-start | bytes 196616 | tf_op jit(solution)/shard_map/ppermute | solution.py:14
  370.6 1.8 collective-permute-done
  373.3 3.6 collective-permute-start.1
  (125 shorter events, 19.2 us)
Async XLA Ops:
  7.2 5.2 %copy-start.9 = (bf16[1,8,128,2,512]{4,3,2,1,0:T(2,128)(2,1)S(1)}, bf16[1,8,128,2,512]{4,3,2,1,0:T(2,128)(2,1)}, u32[]{:S(2)}) copy-start(bf16[1,8,128,2,512]{4,3,2,1,0:T(2,128)(2,1)} %param.8) | copy-start | bytes 6291460
  7.2 88.3 %all-gather.3.cloned.1.call-start = ((), (), s32[]{:S(2)}) async-start(), calls=%async_computation.2 | async-start | bytes 8650752 | tf_op jit(solution)/shard_map/all_gather | solution.py:62
  9.4 166.1 %all-gather.5.cloned.1.call-start = ((), (), s32[]{:S(2)}) async-start(), calls=%async_computation.3 | async-start | bytes 1081344 | tf_op jit(solution)/shard_map/all_gather | solution.py:113
  102.1 2.5 copy-start.4
  102.4 2.2 copy-start.2
  105.1 3.0 copy-start.11
  183.5 8.8 %copy-start.10 = (bf16[8,64,4,128]{3,2,1,0:T(4,128)(2,1)S(1)}, bf16[8,64,4,128]{3,2,1,0:T(4,128)(2,1)}, u32[]{:S(2)}) copy-start(bf16[8,64,4,128]{3,2,1,0:T(4,128)(2,1)} %get-tuple-element.39) | copy-start | bytes 1572868
  183.5 176.5 %all-to-all-start = ((bf16[32,64,512]{2,1,0:T(8,128)(2,1)}), bf16[32,64,512]{2,1,0:T(8,128)(2,1)}, u32[]{:S(2)}, u32[]{:S(2)}) async-start(bf16[32,64,512]{2,1,0:T(8,128)(2,1)} %select_select_fusion), calls=%async_computation | async-start | bytes 4194304 | tf_op jit(solution)/shard_map/all_to_all | solution.py:43
  192.1 180.4 %reduce-scatter.2.cloned.1.call-start = ((), (), s32[]{:S(2)}) async-start(), calls=%async_computation.4 | async-start | bytes 4325376 | tf_op jit(solution)/shard_map/reduce_scatter | solution.py:171
  192.1 1.9 copy-start.3
  193.1 1.0 copy-start
  199.9 1.0 copy-start.5
  199.9 3.0 copy-start.1
  201.9 134.8 %copy-start.7 = (bf16[8,1,64,4,128]{4,3,2,0,1:T(4,128)(2,1)S(1)}, bf16[8,1,64,4,128]{4,3,2,0,1:T(4,128)(2,1)}, u32[]{:S(2)}) copy-start(bf16[8,1,64,4,128]{4,3,2,0,1:T(4,128)(2,1)} %squeeze.45) | copy-start | bytes 1572868
  202.9 133.8 %copy-start.8 = (bf16[8,1,64,4,128]{4,3,2,0,1:T(4,128)(2,1)S(1)}, bf16[8,1,64,4,128]{4,3,2,0,1:T(4,128)(2,1)}, u32[]{:S(2)}) copy-start(bf16[8,1,64,4,128]{4,3,2,0,1:T(4,128)(2,1)} %squeeze.44) | copy-start | bytes 1572868
  204.4 143.1 %copy-start.12 = (f32[2]{0:T(128)S(1)}, f32[2]{0:T(128)}, u32[]{:S(2)}) copy-start(f32[2]{0:T(128)} %constant.197.clone) | copy-start | bytes 28
  350.9 6.3 %copy-start.6 = (f32[256,769]{1,0:T(8,128)S(1)}, f32[256,769]{1,0:T(8,128)}, u32[]{:S(2)}) copy-start(f32[256,769]{1,0:T(8,128)} %slice.116) | copy-start | bytes 2362372
  350.9 7.3 %slice-start = ((f32[256,769]{1,0:T(8,128)}), f32[256,768]{1,0:T(8,128)S(1)}, s32[]{:S(2)}) async-start(f32[256,769]{1,0:T(8,128)} %slice.116), calls=%async_computation.5 | async-start | bytes 1572864 | tf_op jit(solution)/shard_map/slice | solution.py:133
  363.0 9.5 %collective-permute-start = (bf16[64,512]{1,0:T(8,128)(2,1)S(1)}, bf16[64,512]{1,0:T(8,128)(2,1)S(1)}, u32[]{:S(2)}, u32[]{:S(2)}) collective-permute-start(bf16[64,512]{1,0:T(8,128)(2,1)S(1)} %bitcast.180), channel_id=1, source_target_pairs={{0,4},{4,8},{8,12},{12,16},{16,20},{20,24},{24,28},{28,32},{32,36}... | collective-permute-start | bytes 196616 | tf_op jit(solution)/shard_map/ppermute | solution.py:14
  373.3 5.2 %collective-permute-start.1 = (bf16[64,512]{1,0:T(8,128)(2,1)S(1)}, bf16[64,512]{1,0:T(8,128)(2,1)S(1)}, u32[]{:S(2)}, u32[]{:S(2)}) collective-permute-start(bf16[64,512]{1,0:T(8,128)(2,1)S(1)} %slice_bitcast_fusion.1), channel_id=1, source_target_pairs={{0,4},{4,8},{8,12},{12,16},{16,20},{20,24},{24,28},{28,32},{32,36}... | collective-permute-start | bytes 196616 | tf_op jit(solution)/shard_map/ppermute | solution.py:14
Sparse Core Ops, SparseCore 0:
  10.1 85.2 all-gather.2
  108.2 67.1 all-gather.4
  200.0 152.4 reduce-scatter.1
